TPU v7x, 1024 devices: a whole 4x8x16 slice. The times are simulated.
1024 devices in a mesh: seq: 64 (over y_hi, z), chan: 16 (over y_lo, x, core).
Axes of the slice: x: 4, y: 8 (y_hi: 4, y_lo: 2; y = y_hi * 2 + y_lo), z: 16, core: 2. Of those that a mesh axis runs over, the one named last changes fastest.
Arguments:
- query_gate: float32 [64, 524288], P('chan', 'seq'), may hold values from -6 to 6
- key_gate: float32 [64, 524288], P('chan', 'seq'), may hold values from -6 to 6
- value_input: float32 [64, 524288], P('chan', 'seq'), may hold values from -6 to 6
- filter_taps: float32 [4, 524288], P(None, ('seq', 'chan')), may hold values from -2 to 2
- cotangent: float32 [64, 524288], P('chan', 'seq'), may hold values from -6 to 6
Outputs:
- query_grad: float32 [64, 524288], P('chan', 'seq')
- key_grad: float32 [64, 524288], P('chan', 'seq')
- value_grad: float32 [64, 524288], P('chan', 'seq')
All inputs are finite; a program needn't handle non-finite values.
Results may differ from a plain program's by a relative error of at most 0.00013.
Values sent between devices are 32-bit elements; how exact they have to be, the bound alone decides.
No kernel may reach another device: no remote copies, remote signals or barrier semaphores. Data moves between devices by JAX's collectives and lax.ppermute only.
A program may use at most 32 MiB of HBM per device.

v0:
```python
from functools import partial
import math

import jax
import jax.numpy as jnp
from jax import lax
from jax.sharding import PartitionSpec as P


def phase_table(row_count, column_count, offset, period, direction):
    row_index = lax.broadcasted_iota(jnp.int32, (row_count, column_count), 0)
    column_index = lax.broadcasted_iota(jnp.int32, (row_count, column_count), 1)
    phases = row_index * (column_index + offset) % period
    angles = phases.astype(jnp.float32) * (direction * 2.0 * math.pi / period)
    return (jnp.cos(angles), jnp.sin(angles))


def complex_mix(formula, table_real, table_imag, data_real, data_imag):
    product = partial(jnp.einsum, formula, precision=lax.Precision.HIGHEST)
    return (
        product(table_real, data_real) - product(table_imag, data_imag),
        product(table_real, data_imag) + product(table_imag, data_real),
    )


def regroup_tokens(signal):
    return lax.all_to_all(signal, "seq", split_axis=1, concat_axis=1, tiled=True)


def regroup_spectrum(part_real, part_imag):
    return (
        lax.all_to_all(part_real, "seq", split_axis=1, concat_axis=1, tiled=True),
        lax.all_to_all(part_imag, "seq", split_axis=1, concat_axis=1, tiled=True),
    )


def finish_forward(moved_real, moved_imag, blocks, width, tokens):
    outer_real, outer_imag = phase_table(blocks, blocks, 0, blocks, -1.0)
    coarse_real, coarse_imag = complex_mix(
        "ur,crjq->cujq", outer_real, outer_imag, moved_real, moved_imag
    )
    shift_real, shift_imag = phase_table(blocks, width, 0, tokens, -1.0)
    shift_real = shift_real[None, :, None, :]
    shift_imag = shift_imag[None, :, None, :]
    twisted_real = coarse_real * shift_real - coarse_imag * shift_imag
    twisted_imag = coarse_real * shift_imag + coarse_imag * shift_real
    inner_real, inner_imag = phase_table(width, width, 0, width, -1.0)
    return complex_mix("qv,cujq->cujv", inner_real, inner_imag, twisted_real, twisted_imag)


def start_inverse(spectrum_real, spectrum_imag, blocks, width, tokens):
    inner_real, inner_imag = phase_table(width, width, 0, width, 1.0)
    fine_real, fine_imag = complex_mix(
        "vq,cujv->cujq", inner_real, inner_imag, spectrum_real, spectrum_imag
    )
    shift_real, shift_imag = phase_table(blocks, width, 0, tokens, 1.0)
    shift_real = shift_real[None, :, None, :]
    shift_imag = shift_imag[None, :, None, :]
    untwisted_real = fine_real * shift_real - fine_imag * shift_imag
    untwisted_imag = fine_real * shift_imag + fine_imag * shift_real
    outer_real, outer_imag = phase_table(blocks, blocks, 0, blocks, 1.0)
    return complex_mix("ru,cujq->crjq", outer_real, outer_imag, untwisted_real, untwisted_imag)


def forward_spectrum(signal):
    count, tokens = signal.shape
    blocks = lax.axis_size("seq")
    width = tokens // blocks
    freqs = 2 * blocks
    period = freqs * tokens
    rank = lax.axis_index("seq")
    gathered = regroup_tokens(signal.reshape(count, blocks, width))
    product = partial(jnp.einsum, "kp,cpq->ckq", precision=lax.Precision.HIGHEST)
    anchor = rank * width
    first_real, first_imag = phase_table(freqs, blocks, 0, freqs, -1.0)
    mixed_real = product(first_real, gathered)
    mixed_imag = product(first_imag, gathered)
    turn_real, turn_imag = phase_table(freqs, width, anchor, period, -1.0)
    moved_real, moved_imag = regroup_spectrum(
        mixed_real * turn_real - mixed_imag * turn_imag,
        mixed_real * turn_imag + mixed_imag * turn_real,
    )
    moved_real = moved_real.reshape(count, blocks, 2, width)
    moved_imag = moved_imag.reshape(count, blocks, 2, width)
    return finish_forward(moved_real, moved_imag, blocks, width, tokens)


def inverse_spectrum(spectrum_real, spectrum_imag):
    count, blocks, per_device, width = spectrum_real.shape
    tokens = blocks * width
    freqs = 2 * blocks
    period = freqs * tokens
    rank = lax.axis_index("seq")
    spread_real, spread_imag = start_inverse(spectrum_real, spectrum_imag, blocks, width, tokens)
    product = partial(jnp.einsum, "kp,ckq->cpq", precision=lax.Precision.HIGHEST)
    anchor = rank * width
    moved_real, moved_imag = regroup_spectrum(
        spread_real.reshape(count, blocks * per_device, width),
        spread_imag.reshape(count, blocks * per_device, width),
    )
    turn_real, turn_imag = phase_table(freqs, width, anchor, period, 1.0)
    level_real = moved_real * turn_real - moved_imag * turn_imag
    level_imag = moved_real * turn_imag + moved_imag * turn_real
    first_real, first_imag = phase_table(freqs, blocks, 0, freqs, 1.0)
    rebuilt = (product(first_real, level_real) - product(first_imag, level_imag)) * (1.0 / period)
    return regroup_tokens(rebuilt).reshape(count, tokens)


def on_device(query_gate, key_gate, value_input, filter_taps, cotangent):
    block_taps = lax.all_gather(filter_taps, "chan", axis=1, tiled=True)
    filter_real, filter_imag = forward_spectrum(block_taps)
    gated = key_gate * value_input
    weighted = cotangent * query_gate
    gated_real, gated_imag = forward_spectrum(gated)
    convolved = inverse_spectrum(
        gated_real * filter_real - gated_imag * filter_imag,
        gated_real * filter_imag + gated_imag * filter_real,
    )
    weighted_real, weighted_imag = forward_spectrum(weighted)
    gated_grad = inverse_spectrum(
        weighted_real * filter_real + weighted_imag * filter_imag,
        weighted_imag * filter_real - weighted_real * filter_imag,
    )
    return (cotangent * convolved, gated_grad * value_input, gated_grad * key_gate)


def solution(mesh):
    in_specs = (
        P("chan", "seq"),
        P("chan", "seq"),
        P("chan", "seq"),
        P(None, ("seq", "chan")),
        P("chan", "seq"),
    )
    out_specs = (P("chan", "seq"), P("chan", "seq"), P("chan", "seq"))
    return jax.shard_map(
        on_device, mesh=mesh, in_specs=in_specs, out_specs=out_specs, check_vma=False
    )
```

profile of v0, /device:TPU:8, one launch (start us, length us, event | category | flops | bytes accessed | tf_op | source)
XLA Modules:
  0.0 473.1 jit_solution(17470145111232782204)
XLA Ops:
  2.3 24.3 %all-to-all-start = ((f32[4,64,128]{2,0,1:T(4,128)}), f32[4,64,128]{2,0,1:T(4,128)S(1)}, u32[]{:S(2)}, u32[]{:S(2)}) async-start(f32[4,64,128]{2,0,1:T(4,128)} %multiply_bitcast_fusion.1), calls=%async_computation | async-start | bytes 262144 | tf_op jit(solution)/shard_map/all_to_all | solution.py:27
  27.3 18.0 %all-to-all-done = f32[4,64,128]{2,0,1:T(4,128)S(1)} async-done(((f32[4,64,128]{2,0,1:T(4,128)}), f32[4,64,128]{2,0,1:T(4,128)S(1)}, u32[]{:S(2)}, u32[]{:S(2)}) %all-to-all-start) | async-done | bytes 131104 | tf_op jit(solution)/shard_map/all_to_all | solution.py:27
  51.6 21.4 %all_gather.3 = f32[4,8192]{1,0:T(4,128)} all-gather(f32[4,512]{1,0:T(4,128)S(1)} %copy-done.4), channel_id=1, replica_groups=mesh['seq'=64,'chan'=16] {'chan'}, dimensions={1}, use_global_device_ids=true | all-gather | bytes 139264 | tf_op jit(solution)/shard_map/all_gather | solution.py:110
  73.6 17.4 %all-to-all-start.3 = ((f32[4,64,128]{2,0,1:T(4,128)}), f32[4,64,128]{2,0,1:T(4,128)S(1)}, u32[]{:S(2)}, u32[]{:S(2)}) async-start(f32[4,64,128]{2,0,1:T(4,128)} %bitcast.19), calls=%async_computation.3 | async-start | bytes 262144 | tf_op jit(solution)/shard_map/all_to_all | solution.py:27
  93.7 15.7 %all-to-all-done.3 = f32[4,64,128]{2,0,1:T(4,128)S(1)} async-done(((f32[4,64,128]{2,0,1:T(4,128)}), f32[4,64,128]{2,0,1:T(4,128)S(1)}, u32[]{:S(2)}, u32[]{:S(2)}) %all-to-all-start.3) | async-done | bytes 131104 | tf_op jit(solution)/shard_map/all_to_all | solution.py:27
  116.1 20.2 %all-to-all-done.2 = f32[4,128,128]{2,0,1:T(4,128)S(1)} async-done(((f32[4,128,128]{2,0,1:T(4,128)}), f32[4,128,128]{2,0,1:T(4,128)S(1)}, u32[]{:S(2)}, u32[]{:S(2)}) %all-to-all-start.2) | async-done | bytes 262176 | tf_op jit(solution)/shard_map/all_to_all | solution.py:33
  136.3 8.3 %all-to-all-start.1 = ((f32[4,128,128]{2,0,1:T(4,128)}), f32[4,128,128]{2,0,1:T(4,128)S(1)}, u32[]{:S(2)}, u32[]{:S(2)}) async-start(f32[4,128,128]{2,0,1:T(4,128)} %copy.88), calls=%async_computation.1 | async-start | bytes 524288 | tf_op jit(solution)/shard_map/all_to_all | solution.py:32
  146.6 18.9 %all-to-all-done.1 = f32[4,128,128]{2,0,1:T(4,128)S(1)} async-done(((f32[4,128,128]{2,0,1:T(4,128)}), f32[4,128,128]{2,0,1:T(4,128)S(1)}, u32[]{:S(2)}, u32[]{:S(2)}) %all-to-all-start.1) | async-done | bytes 262176 | tf_op jit(solution)/shard_map/all_to_all | solution.py:32
  165.5 8.1 %all-to-all-start.4 = ((f32[4,128,128]{2,0,1:T(4,128)}), f32[4,128,128]{2,0,1:T(4,128)S(1)}, u32[]{:S(2)}, u32[]{:S(2)}) async-start(f32[4,128,128]{2,0,1:T(4,128)} %copy.98), calls=%async_computation.4 | async-start | bytes 524288 | tf_op jit(solution)/shard_map/all_to_all | solution.py:32
  174.6 20.0 %all-to-all-done.4 = f32[4,128,128]{2,0,1:T(4,128)S(1)} async-done(((f32[4,128,128]{2,0,1:T(4,128)}), f32[4,128,128]{2,0,1:T(4,128)S(1)}, u32[]{:S(2)}, u32[]{:S(2)}) %all-to-all-start.4) | async-done | bytes 262176 | tf_op jit(solution)/shard_map/all_to_all | solution.py:32
  194.6 20.4 %all-to-all-start.5 = ((f32[4,128,128]{2,0,1:T(4,128)}), f32[4,128,128]{2,0,1:T(4,128)S(1)}, u32[]{:S(2)}, u32[]{:S(2)}) async-start(f32[4,128,128]{2,0,1:T(4,128)} %copy.101), calls=%async_computation.5 | async-start | bytes 524288 | tf_op jit(solution)/shard_map/all_to_all | solution.py:33
  218.7 17.1 %all-to-all-done.5 = f32[4,128,128]{2,0,1:T(4,128)S(1)} async-done(((f32[4,128,128]{2,0,1:T(4,128)}), f32[4,128,128]{2,0,1:T(4,128)S(1)}, u32[]{:S(2)}, u32[]{:S(2)}) %all-to-all-start.5) | async-done | bytes 262176 | tf_op jit(solution)/shard_map/all_to_all | solution.py:33
  235.8 7.9 %all-to-all-start.11 = ((f32[4,128,128]{2,0,1:T(4,128)}), f32[4,128,128]{2,0,1:T(4,128)S(1)}, u32[]{:S(2)}, u32[]{:S(2)}) async-start(f32[4,128,128]{2,0,1:T(4,128)} %copy.118), calls=%async_computation.11 | async-start | bytes 524288 | tf_op jit(solution)/shard_map/all_to_all | solution.py:33
  246.4 18.3 %all-to-all-done.11 = f32[4,128,128]{2,0,1:T(4,128)S(1)} async-done(((f32[4,128,128]{2,0,1:T(4,128)}), f32[4,128,128]{2,0,1:T(4,128)S(1)}, u32[]{:S(2)}, u32[]{:S(2)}) %all-to-all-start.11) | async-done | bytes 262176 | tf_op jit(solution)/shard_map/all_to_all | solution.py:33
  264.7 7.9 %all-to-all-start.10 = ((f32[4,128,128]{2,0,1:T(4,128)}), f32[4,128,128]{2,0,1:T(4,128)S(1)}, u32[]{:S(2)}, u32[]{:S(2)}) async-start(f32[4,128,128]{2,0,1:T(4,128)} %copy.115), calls=%async_computation.10 | async-start | bytes 524288 | tf_op jit(solution)/shard_map/all_to_all | solution.py:32
  275.6 18.0 %all-to-all-done.10 = f32[4,128,128]{2,0,1:T(4,128)S(1)} async-done(((f32[4,128,128]{2,0,1:T(4,128)}), f32[4,128,128]{2,0,1:T(4,128)S(1)}, u32[]{:S(2)}, u32[]{:S(2)}) %all-to-all-start.10) | async-done | bytes 262176 | tf_op jit(solution)/shard_map/all_to_all | solution.py:32
  305.1 7.9 %all-to-all-start.6 = ((f32[4,128,128]{2,0,1:T(4,128)}), f32[4,128,128]{2,0,1:T(4,128)S(1)}, u32[]{:S(2)}, u32[]{:S(2)}) async-start(f32[4,128,128]{2,0,1:T(4,128)} %copy.107), calls=%async_computation.6 | async-start | bytes 524288 | tf_op jit(solution)/shard_map/all_to_all | solution.py:32
  315.9 18.1 %all-to-all-done.6 = f32[4,128,128]{2,0,1:T(4,128)S(1)} async-done(((f32[4,128,128]{2,0,1:T(4,128)}), f32[4,128,128]{2,0,1:T(4,128)S(1)}, u32[]{:S(2)}, u32[]{:S(2)}) %all-to-all-start.6) | async-done | bytes 262176 | tf_op jit(solution)/shard_map/all_to_all | solution.py:32
  334.0 7.9 %all-to-all-start.7 = ((f32[4,128,128]{2,0,1:T(4,128)}), f32[4,128,128]{2,0,1:T(4,128)S(1)}, u32[]{:S(2)}, u32[]{:S(2)}) async-start(f32[4,128,128]{2,0,1:T(4,128)} %copy.109), calls=%async_computation.7 | async-start | bytes 524288 | tf_op jit(solution)/shard_map/all_to_all | solution.py:33
  346.0 17.3 %all-to-all-done.7 = f32[4,128,128]{2,0,1:T(4,128)S(1)} async-done(((f32[4,128,128]{2,0,1:T(4,128)}), f32[4,128,128]{2,0,1:T(4,128)S(1)}, u32[]{:S(2)}, u32[]{:S(2)}) %all-to-all-start.7) | async-done | bytes 262176 | tf_op jit(solution)/shard_map/all_to_all | solution.py:33
  372.3 19.8 %all-to-all-done.12 = f32[4,128,128]{2,0,1:T(4,128)S(1)} async-done(((f32[4,128,128]{2,0,1:T(4,128)}), f32[4,128,128]{2,0,1:T(4,128)S(1)}, u32[]{:S(2)}, u32[]{:S(2)}) %all-to-all-start.12) | async-done | bytes 262176 | tf_op jit(solution)/shard_map/all_to_all | solution.py:32
  392.1 28.4 %all_to_all.75 = f32[4,128,128]{2,0,1:T(4,128)S(1)} all-to-all(f32[4,128,128]{2,0,1:T(4,128)S(1)} %copy.126), channel_id=1, replica_groups=mesh['seq'=64,'chan'=16] {'seq'}, dimensions={1} | all-to-all | bytes 524288 | tf_op jit(solution)/shard_map/all_to_all | solution.py:33
  431.8 16.7 %all-to-all-done.14 = f32[4,64,128]{2,0,1:T(4,128)S(1)} async-done(((f32[4,64,128]{2,0,1:T(4,128)}), f32[4,64,128]{2,0,1:T(4,128)S(1)}, u32[]{:S(2)}, u32[]{:S(2)}) %all-to-all-start.14) | async-done | bytes 131104 | tf_op jit(solution)/shard_map/all_to_all | solution.py:27
  454.2 17.8 %all-to-all-done.8 = f32[4,64,128]{2,0,1:T(4,128)S(1)} async-done(((f32[4,64,128]{2,0,1:T(4,128)}), f32[4,64,128]{2,0,1:T(4,128)S(1)}, u32[]{:S(2)}, u32[]{:S(2)}) %all-to-all-start.8) | async-done | bytes 131104 | tf_op jit(solution)/shard_map/all_to_all | solution.py:27
  (99 shorter events, 75.4 us)
Async XLA Ops:
  2.3 24.3 %copy-start.2 = (f32[4,8192]{1,0:T(4,128)S(1)}, f32[4,8192]{1,0:T(4,128)}, u32[]{:S(2)}) copy-start(f32[4,8192]{1,0:T(4,128)} %param.9) | copy-start | bytes 393220
  2.3 24.3 %copy-start.3 = (f32[4,8192]{1,0:T(4,128)S(1)}, f32[4,8192]{1,0:T(4,128)}, u32[]{:S(2)}) copy-start(f32[4,8192]{1,0:T(4,128)} %param.5) | copy-start | bytes 393220
  2.3 43.0 %all-to-all-start = ((f32[4,64,128]{2,0,1:T(4,128)}), f32[4,64,128]{2,0,1:T(4,128)S(1)}, u32[]{:S(2)}, u32[]{:S(2)}) async-start(f32[4,64,128]{2,0,1:T(4,128)} %multiply_bitcast_fusion.1), calls=%async_computation | async-start | bytes 262144 | tf_op jit(solution)/shard_map/all_to_all | solution.py:27
  45.3 28.3 %all-to-all-start.9 = ((f32[4,64,128]{2,0,1:T(4,128)}), f32[4,64,128]{2,0,1:T(4,128)S(1)}, u32[]{:S(2)}, u32[]{:S(2)}) async-start(f32[4,64,128]{2,0,1:T(4,128)} %multiply_bitcast_fusion), calls=%async_computation.9 | async-start | bytes 262144 | tf_op jit(solution)/shard_map/all_to_all | solution.py:27
  50.9 0.7 copy-start.4
  73.6 35.9 %all-to-all-start.3 = ((f32[4,64,128]{2,0,1:T(4,128)}), f32[4,64,128]{2,0,1:T(4,128)S(1)}, u32[]{:S(2)}, u32[]{:S(2)}) async-start(f32[4,64,128]{2,0,1:T(4,128)} %bitcast.19), calls=%async_computation.3 | async-start | bytes 262144 | tf_op jit(solution)/shard_map/all_to_all | solution.py:27
  109.5 26.8 %all-to-all-start.2 = ((f32[4,128,128]{2,0,1:T(4,128)}), f32[4,128,128]{2,0,1:T(4,128)S(1)}, u32[]{:S(2)}, u32[]{:S(2)}) async-start(f32[4,128,128]{2,0,1:T(4,128)} %copy.91), calls=%async_computation.2 | async-start | bytes 524288 | tf_op jit(solution)/shard_map/all_to_all | solution.py:33
  136.3 29.2 %all-to-all-start.1 = ((f32[4,128,128]{2,0,1:T(4,128)}), f32[4,128,128]{2,0,1:T(4,128)S(1)}, u32[]{:S(2)}, u32[]{:S(2)}) async-start(f32[4,128,128]{2,0,1:T(4,128)} %copy.88), calls=%async_computation.1 | async-start | bytes 524288 | tf_op jit(solution)/shard_map/all_to_all | solution.py:32
  165.5 29.1 %all-to-all-start.4 = ((f32[4,128,128]{2,0,1:T(4,128)}), f32[4,128,128]{2,0,1:T(4,128)S(1)}, u32[]{:S(2)}, u32[]{:S(2)}) async-start(f32[4,128,128]{2,0,1:T(4,128)} %copy.98), calls=%async_computation.4 | async-start | bytes 524288 | tf_op jit(solution)/shard_map/all_to_all | solution.py:32
  194.6 41.2 %all-to-all-start.5 = ((f32[4,128,128]{2,0,1:T(4,128)}), f32[4,128,128]{2,0,1:T(4,128)S(1)}, u32[]{:S(2)}, u32[]{:S(2)}) async-start(f32[4,128,128]{2,0,1:T(4,128)} %copy.101), calls=%async_computation.5 | async-start | bytes 524288 | tf_op jit(solution)/shard_map/all_to_all | solution.py:33
  235.8 28.9 %all-to-all-start.11 = ((f32[4,128,128]{2,0,1:T(4,128)}), f32[4,128,128]{2,0,1:T(4,128)S(1)}, u32[]{:S(2)}, u32[]{:S(2)}) async-start(f32[4,128,128]{2,0,1:T(4,128)} %copy.118), calls=%async_computation.11 | async-start | bytes 524288 | tf_op jit(solution)/shard_map/all_to_all | solution.py:33
  264.7 28.9 %all-to-all-start.10 = ((f32[4,128,128]{2,0,1:T(4,128)}), f32[4,128,128]{2,0,1:T(4,128)S(1)}, u32[]{:S(2)}, u32[]{:S(2)}) async-start(f32[4,128,128]{2,0,1:T(4,128)} %copy.115), calls=%async_computation.10 | async-start | bytes 524288 | tf_op jit(solution)/shard_map/all_to_all | solution.py:32
  305.1 28.9 %all-to-all-start.6 = ((f32[4,128,128]{2,0,1:T(4,128)}), f32[4,128,128]{2,0,1:T(4,128)S(1)}, u32[]{:S(2)}, u32[]{:S(2)}) async-start(f32[4,128,128]{2,0,1:T(4,128)} %copy.107), calls=%async_computation.6 | async-start | bytes 524288 | tf_op jit(solution)/shard_map/all_to_all | solution.py:32
  334.0 29.3 %all-to-all-start.7 = ((f32[4,128,128]{2,0,1:T(4,128)}), f32[4,128,128]{2,0,1:T(4,128)S(1)}, u32[]{:S(2)}, u32[]{:S(2)}) async-start(f32[4,128,128]{2,0,1:T(4,128)} %copy.109), calls=%async_computation.7 | async-start | bytes 524288 | tf_op jit(solution)/shard_map/all_to_all | solution.py:33
  363.3 28.8 %all-to-all-start.12 = ((f32[4,128,128]{2,0,1:T(4,128)}), f32[4,128,128]{2,0,1:T(4,128)S(1)}, u32[]{:S(2)}, u32[]{:S(2)}) async-start(f32[4,128,128]{2,0,1:T(4,128)} %copy.124), calls=%async_computation.12 | async-start | bytes 524288 | tf_op jit(solution)/shard_map/all_to_all | solution.py:32
  422.4 26.1 %all-to-all-start.14 = ((f32[4,64,128]{2,0,1:T(4,128)}), f32[4,64,128]{2,0,1:T(4,128)S(1)}, u32[]{:S(2)}, u32[]{:S(2)}) async-start(f32[4,64,128]{2,0,1:T(4,128)} %copy.129), calls=%async_computation.14 | async-start | bytes 262144 | tf_op jit(solution)/shard_map/all_to_all | solution.py:27
  431.8 21.6 %copy-start = (f32[4,8192]{1,0:T(4,128)S(1)}, f32[4,8192]{1,0:T(4,128)}, u32[]{:S(2)}) copy-start(f32[4,8192]{1,0:T(4,128)} %param.6) | copy-start | bytes 393220
  431.8 21.7 %copy-start.1 = (f32[4,8192]{1,0:T(4,128)S(1)}, f32[4,8192]{1,0:T(4,128)}, u32[]{:S(2)}) copy-start(f32[4,8192]{1,0:T(4,128)} %param.7) | copy-start | bytes 393220
  448.5 23.5 %all-to-all-start.8 = ((f32[4,64,128]{2,0,1:T(4,128)}), f32[4,64,128]{2,0,1:T(4,128)S(1)}, u32[]{:S(2)}, u32[]{:S(2)}) async-start(f32[4,64,128]{2,0,1:T(4,128)} %copy.112), calls=%async_computation.8 | async-start | bytes 262144 | tf_op jit(solution)/shard_map/all_to_all | solution.py:27
where the time goes:
time: 483 us; the launch traced here: 473 us
  waiting for transfers between devices  236 us (49%)
  starting transfers between devices  141 us (29%)
  blocking collectives  49.8 us (10%)
  matrix products  28.6 us (6%)
  local copies, waits for them, and re-layouts  11.1 us (2%)
    all_to_all x5, waiting for transfers between devices, regroup_spectrum(): lax.all_to_all(part_real, 'seq', split_axis=1, concat_axis=1, tiled=True)  94.8 us
    all_to_all x4, waiting for transfers between devices, regroup_spectrum(): lax.all_to_all(part_imag, 'seq', split_axis=1, concat_axis=1, tiled=True)  72.9 us
    all_to_all x5, waiting for transfers between devices, regroup_tokens(): lax.all_to_all(signal, 'seq', split_axis=1, concat_axis=1, tiled=True)  68.2 us
    all_to_all x5, starting transfers between devices, regroup_tokens(): lax.all_to_all(signal, 'seq', split_axis=1, concat_axis=1, tiled=True)  59.4 us
    all_to_all x4, starting transfers between devices, regroup_spectrum(): lax.all_to_all(part_imag, 'seq', split_axis=1, concat_axis=1, tiled=True)  42 us
    all_to_all x5, starting transfers between devices, regroup_spectrum(): lax.all_to_all(part_real, 'seq', split_axis=1, concat_axis=1, tiled=True)  39.8 us
    all_to_all x1, blocking collectives, regroup_spectrum(): lax.all_to_all(part_imag, 'seq', split_axis=1, concat_axis=1, tiled=True)  28.4 us
    all_gather x1, blocking collectives, on_device(): block_taps = lax.all_gather(filter_taps, 'chan', axis=1, tiled=True)  21.4 us
  transfers between devices with their start and end apart: 14, of which 13 were waited for; matrix products, arithmetic and copies ran while one was open for 6% of the time, Pallas kernels for 0%

commit v1 on v0

--- a/solution.py
+++ b/solution.py
@@ -28,10 +28,15 @@
 
 
 def regroup_spectrum(part_real, part_imag):
-    return (
-        lax.all_to_all(part_real, "seq", split_axis=1, concat_axis=1, tiled=True),
-        lax.all_to_all(part_imag, "seq", split_axis=1, concat_axis=1, tiled=True),
+    count = part_real.shape[0]
+    moved = lax.all_to_all(
+        jnp.concatenate([part_real, part_imag], axis=0),
+        "seq",
+        split_axis=1,
+        concat_axis=1,
+        tiled=True,
     )
+    return moved[:count], moved[count:]
 
 
 def finish_forward(moved_real, moved_imag, blocks, width, tokens):
@@ -108,19 +113,39 @@
 
 def on_device(query_gate, key_gate, value_input, filter_taps, cotangent):
     block_taps = lax.all_gather(filter_taps, "chan", axis=1, tiled=True)
-    filter_real, filter_imag = forward_spectrum(block_taps)
     gated = key_gate * value_input
     weighted = cotangent * query_gate
-    gated_real, gated_imag = forward_spectrum(gated)
-    convolved = inverse_spectrum(
-        gated_real * filter_real - gated_imag * filter_imag,
-        gated_real * filter_imag + gated_imag * filter_real,
+    rows = gated.shape[0]
+    filters = block_taps.shape[0]
+    all_real, all_imag = forward_spectrum(
+        jnp.concatenate([block_taps, gated, weighted], axis=0)
     )
-    weighted_real, weighted_imag = forward_spectrum(weighted)
-    gated_grad = inverse_spectrum(
-        weighted_real * filter_real + weighted_imag * filter_imag,
-        weighted_imag * filter_real - weighted_real * filter_imag,
+    filter_real, filter_imag = all_real[:filters], all_imag[:filters]
+    gated_real = all_real[filters:filters + rows]
+    gated_imag = all_imag[filters:filters + rows]
+    weighted_real = all_real[filters + rows:]
+    weighted_imag = all_imag[filters + rows:]
+    reps = rows // filters
+    filter_real = jnp.tile(filter_real, (reps, 1, 1, 1))
+    filter_imag = jnp.tile(filter_imag, (reps, 1, 1, 1))
+    both = inverse_spectrum(
+        jnp.concatenate(
+            [
+                gated_real * filter_real - gated_imag * filter_imag,
+                weighted_real * filter_real + weighted_imag * filter_imag,
+            ],
+            axis=0,
+        ),
+        jnp.concatenate(
+            [
+                gated_real * filter_imag + gated_imag * filter_real,
+                weighted_imag * filter_real - weighted_real * filter_imag,
+            ],
+            axis=0,
+        ),
     )
+    convolved = both[:rows]
+    gated_grad = both[rows:]
     return (cotangent * convolved, gated_grad * value_input, gated_grad * key_gate)
 
 

time: 483 us -> 283 us (0.59)
  the two profiles are of different devices: /device:TPU:8 before, /device:TPU:16 now
where the time goes in v1:
time: 283 us
  blocking collectives  114 us (40%)
  waiting for transfers between devices  107 us (38%)
  starting transfers between devices  33 us (12%)
  matrix products  18.6 us (7%)
  local copies, waits for them, and re-layouts  4.43 us (2%)
  other arithmetic  4.19 us (1%)
    all_to_all x1, waiting for transfers between devices, regroup_spectrum(): lax.all_to_all(jnp.concatenate([part_real, part_imag], axis=0), 'seq', sp...  75.5 us
    all_to_all x1, blocking collectives, regroup_spectrum(): lax.all_to_all(jnp.concatenate([part_real, part_imag], axis=0), 'seq', sp...  63 us
    all_to_all x1, waiting for transfers between devices, regroup_tokens(): lax.all_to_all(signal, 'seq', split_axis=1, concat_axis=1, tiled=True)  31.5 us
    all_to_all x1, blocking collectives, regroup_tokens(): lax.all_to_all(signal, 'seq', split_axis=1, concat_axis=1, tiled=True)  31.1 us
    all_to_all x1, starting transfers between devices, regroup_tokens(): lax.all_to_all(signal, 'seq', split_axis=1, concat_axis=1, tiled=True)  24 us
    all_gather x1, blocking collectives, on_device(): block_taps = lax.all_gather(filter_taps, 'chan', axis=1, tiled=True)  20.3 us
    all_to_all x1, starting transfers between devices, regroup_spectrum(): lax.all_to_all(jnp.concatenate([part_real, part_imag], axis=0), 'seq', sp...  9 us
  transfers between devices with their start and end apart: 2, of which 2 were waited for; matrix products, arithmetic and copies ran while one was open for 0% of the time, Pallas kernels for 0%

profile of v1, /device:TPU:16, one launch (start us, length us, event | category | flops | bytes accessed | tf_op | source)
XLA Modules:
  0.0 282.7 jit_solution(3833280351693240147)
XLA Ops:
  0.6 20.3 %all_gather.3 = f32[4,8192]{1,0:T(4,128)S(1)} all-gather(f32[4,512]{1,0:T(4,128)} %param.8), channel_id=1, replica_groups=mesh['seq'=64,'chan'=16] {'chan'}, dimensions={1}, use_global_device_ids=true | all-gather | bytes 139264 | tf_op jit(solution)/shard_map/all_gather | solution.py:115
  20.9 1.0 mul.394
  21.9 1.0 mul.395
  23.2 1.0 copy.42
  24.2 24.0 %all-to-all-start = ((f32[12,64,128]{2,0,1:T(8,128)}), f32[12,64,128]{2,0,1:T(8,128)S(1)}, u32[]{:S(2)}, u32[]{:S(2)}) async-start(f32[12,64,128]{2,0,1:T(8,128)} %copy.42), calls=%async_computation | async-start | bytes 1048576 | tf_op jit(solution)/shard_map/all_to_all | solution.py:27
  48.9 31.5 %all-to-all-done = f32[12,64,128]{2,0,1:T(8,128)S(1)} async-done(((f32[12,64,128]{2,0,1:T(8,128)}), f32[12,64,128]{2,0,1:T(8,128)S(1)}, u32[]{:S(2)}, u32[]{:S(2)}) %all-to-all-start) | async-done | bytes 393248 | tf_op jit(solution)/shard_map/all_to_all | solution.py:27
  80.5 1.5 convolution_bitcast_fusion.1
  82.0 1.5 multiply_subtract_fusion.1
  83.6 1.6 copy.47
  85.2 9.0 %all-to-all-start.1 = ((f32[24,128,128]{2,0,1:T(8,128)}), f32[24,128,128]{2,0,1:T(8,128)S(1)}, u32[]{:S(2)}, u32[]{:S(2)}) async-start(f32[24,128,128]{2,0,1:T(8,128)} %copy.47), calls=%async_computation.1 | async-start | bytes 3145728 | tf_op jit(solution)/shard_map/all_to_all | solution.py:32
  94.5 75.5 %all-to-all-done.1 = f32[24,128,128]{2,0,1:T(8,128)S(1)} async-done(((f32[24,128,128]{2,0,1:T(8,128)}), f32[24,128,128]{2,0,1:T(8,128)S(1)}, u32[]{:S(2)}, u32[]{:S(2)}) %all-to-all-start.1) | async-done | bytes 1572896 | tf_op jit(solution)/shard_map/all_to_all | solution.py:32
  170.5 0.9 fusion.10
  171.7 0.9 fusion.6
  172.6 0.9 fusion.1
  173.6 0.9 fusion
  174.5 1.0 fusion.19
  175.6 1.0 fusion.20
  176.6 1.0 convolution_subtract_fusion
  177.6 1.0 convolution_add_fusion
  180.5 0.8 convolution_subtract_fusion.3
  181.3 1.1 convolution_add_fusion.3
  186.2 63.0 %all_to_all.20 = f32[16,128,128]{2,0,1:T(8,128)S(1)} all-to-all(f32[16,128,128]{2,0,1:T(8,128)S(1)} %pad_maximum_fusion.1), channel_id=1, replica_groups=mesh['seq'=64,'chan'=16] {'seq'}, dimensions={1} | all-to-all | bytes 2097152 | tf_op jit(solution)/shard_map/all_to_all | solution.py:32
  250.8 31.1 %all_to_all.21 = f32[8,64,128]{2,0,1:T(8,128)S(1)} all-to-all(f32[8,64,128]{2,0,1:T(8,128)S(1)} %copy.58), channel_id=1, replica_groups=mesh['seq'=64,'chan'=16] {'seq'}, dimensions={1} | all-to-all | bytes 524288 | tf_op jit(solution)/shard_map/all_to_all | solution.py:27
  281.9 0.8 fusion.24
  (33 shorter events, 9.1 us)
Async XLA Ops:
  24.2 56.3 %all-to-all-start = ((f32[12,64,128]{2,0,1:T(8,128)}), f32[12,64,128]{2,0,1:T(8,128)S(1)}, u32[]{:S(2)}, u32[]{:S(2)}) async-start(f32[12,64,128]{2,0,1:T(8,128)} %copy.42), calls=%async_computation | async-start | bytes 1048576 | tf_op jit(solution)/shard_map/all_to_all | solution.py:27
  85.2 84.8 %all-to-all-start.1 = ((f32[24,128,128]{2,0,1:T(8,128)}), f32[24,128,128]{2,0,1:T(8,128)S(1)}, u32[]{:S(2)}, u32[]{:S(2)}) async-start(f32[24,128,128]{2,0,1:T(8,128)} %copy.47), calls=%async_computation.1 | async-start | bytes 3145728 | tf_op jit(solution)/shard_map/all_to_all | solution.py:32
  249.4 32.5 %copy-start = (f32[4,8192]{1,0:T(4,128)S(1)}, f32[4,8192]{1,0:T(4,128)}, u32[]{:S(2)}) copy-start(f32[4,8192]{1,0:T(4,128)} %param.6) | copy-start | bytes 393220
  249.4 32.5 %copy-start.1 = (f32[4,8192]{1,0:T(4,128)S(1)}, f32[4,8192]{1,0:T(4,128)}, u32[]{:S(2)}) copy-start(f32[4,8192]{1,0:T(4,128)} %param.9) | copy-start | bytes 393220
  249.4 32.5 %copy-start.2 = (f32[4,8192]{1,0:T(4,128)S(1)}, f32[4,8192]{1,0:T(4,128)}, u32[]{:S(2)}) copy-start(f32[4,8192]{1,0:T(4,128)} %param.7) | copy-start | bytes 393220

commit v2 on v1

--- a/solution.py
+++ b/solution.py
@@ -67,6 +67,20 @@
     return complex_mix("ru,cujq->crjq", outer_real, outer_imag, untwisted_real, untwisted_imag)
 
 
+def column_twist(row, blocks, width, period, direction):
+    column_index = lax.broadcasted_iota(jnp.int32, (blocks, width), 0) * width + lax.broadcasted_iota(
+        jnp.int32, (blocks, width), 1
+    )
+    phases = row * column_index % period
+    angles = phases.astype(jnp.float32) * (direction * 2.0 * math.pi / period)
+    return (jnp.cos(angles), jnp.sin(angles))
+
+
+def alternating(count, axis):
+    index = lax.broadcasted_iota(jnp.int32, (count, count), axis)
+    return (1 - 2 * (index % 2)).astype(jnp.float32)
+
+
 def forward_spectrum(signal):
     count, tokens = signal.shape
     blocks = lax.axis_size("seq")
@@ -77,17 +91,30 @@
     gathered = regroup_tokens(signal.reshape(count, blocks, width))
     product = partial(jnp.einsum, "kp,cpq->ckq", precision=lax.Precision.HIGHEST)
     anchor = rank * width
-    first_real, first_imag = phase_table(freqs, blocks, 0, freqs, -1.0)
+    first_real, first_imag = phase_table(blocks, blocks, 0, freqs, -1.0)
+    top_row = lax.broadcasted_iota(jnp.int32, (blocks, blocks), 0) == 0
+    first_real = jnp.where(top_row, 1.0, first_real)
+    first_imag = jnp.where(top_row, alternating(blocks, 1), first_imag)
     mixed_real = product(first_real, gathered)
     mixed_imag = product(first_imag, gathered)
-    turn_real, turn_imag = phase_table(freqs, width, anchor, period, -1.0)
+    turn_real, turn_imag = phase_table(blocks, width, anchor, period, -1.0)
     moved_real, moved_imag = regroup_spectrum(
         mixed_real * turn_real - mixed_imag * turn_imag,
         mixed_real * turn_imag + mixed_imag * turn_real,
     )
-    moved_real = moved_real.reshape(count, blocks, 2, width)
-    moved_imag = moved_imag.reshape(count, blocks, 2, width)
-    return finish_forward(moved_real, moved_imag, blocks, width, tokens)
+    lead = rank == 0
+    edge_real, edge_imag = column_twist(blocks, blocks, width, period, -1.0)
+    low_real = moved_real
+    low_imag = jnp.where(lead, 0.0, moved_imag)
+    high_real = jnp.where(lead, moved_imag * edge_real, 0.0)
+    high_imag = jnp.where(lead, moved_imag * edge_imag, 0.0)
+    return finish_forward(
+        jnp.stack([low_real, high_real], axis=2),
+        jnp.stack([low_imag, high_imag], axis=2),
+        blocks,
+        width,
+        tokens,
+    )
 
 
 def inverse_spectrum(spectrum_real, spectrum_imag):
@@ -97,17 +124,20 @@
     period = freqs * tokens
     rank = lax.axis_index("seq")
     spread_real, spread_imag = start_inverse(spectrum_real, spectrum_imag, blocks, width, tokens)
-    product = partial(jnp.einsum, "kp,ckq->cpq", precision=lax.Precision.HIGHEST)
-    anchor = rank * width
+    own_real, own_imag = column_twist(rank, blocks, width, period, 1.0)
+    edge_real, edge_imag = column_twist(blocks, blocks, width, period, 1.0)
+    low_real = spread_real[:, :, 0] * own_real - spread_imag[:, :, 0] * own_imag
+    low_imag = spread_real[:, :, 0] * own_imag + spread_imag[:, :, 0] * own_real
+    high_real = spread_real[:, :, 1] * edge_real - spread_imag[:, :, 1] * edge_imag
     moved_real, moved_imag = regroup_spectrum(
-        spread_real.reshape(count, blocks * per_device, width),
-        spread_imag.reshape(count, blocks * per_device, width),
+        low_real, jnp.where(rank == 0, high_real, low_imag)
     )
-    turn_real, turn_imag = phase_table(freqs, width, anchor, period, 1.0)
-    level_real = moved_real * turn_real - moved_imag * turn_imag
-    level_imag = moved_real * turn_imag + moved_imag * turn_real
-    first_real, first_imag = phase_table(freqs, blocks, 0, freqs, 1.0)
-    rebuilt = (product(first_real, level_real) - product(first_imag, level_imag)) * (1.0 / period)
+    cos_table, sin_table = phase_table(blocks, blocks, 0, freqs, 1.0)
+    first_column = lax.broadcasted_iota(jnp.int32, (blocks, blocks), 1) == 0
+    real_weight = jnp.where(first_column, 1.0, 2.0 * cos_table)
+    imag_weight = jnp.where(first_column, alternating(blocks, 0), -2.0 * sin_table)
+    product = partial(jnp.einsum, "pk,ckq->cpq", precision=lax.Precision.HIGHEST)
+    rebuilt = (product(real_weight, moved_real) + product(imag_weight, moved_imag)) * (1.0 / period)
     return regroup_tokens(rebuilt).reshape(count, tokens)
 
 

time: 283 us -> 223 us (0.79)
  waiting for transfers between devices: 107 us -> 73.7 us
  blocking collectives: 114 us -> 91.5 us
    all_to_all x1, waiting for transfers between devices: 75.5 us -> 41.6 us  [regroup_spectrum(): lax.all_to_all(jnp.concatenate([part_real, part_imag], axis=0), 'seq', sp...]
    all_to_all x1, blocking collectives: 63 us -> 40.2 us  [regroup_spectrum(): lax.all_to_all(jnp.concatenate([part_real, part_imag], axis=0), 'seq', sp...]
where the time goes in v2:
time: 223 us
  blocking collectives  91.5 us (41%)
  waiting for transfers between devices  73.7 us (33%)
  starting transfers between devices  33 us (15%)
  matrix products  16.8 us (8%)
  other arithmetic  3.42 us (2%)
  local copies, waits for them, and re-layouts  3.26 us (1%)
    all_to_all x1, waiting for transfers between devices, regroup_spectrum(): lax.all_to_all(jnp.concatenate([part_real, part_imag], axis=0), 'seq', sp...  41.6 us
    all_to_all x1, blocking collectives, regroup_spectrum(): lax.all_to_all(jnp.concatenate([part_real, part_imag], axis=0), 'seq', sp...  40.2 us
    all_to_all x1, waiting for transfers between devices, regroup_tokens(): lax.all_to_all(signal, 'seq', split_axis=1, concat_axis=1, tiled=True)  32.1 us
    all_to_all x1, blocking collectives, regroup_tokens(): lax.all_to_all(signal, 'seq', split_axis=1, concat_axis=1, tiled=True)  30.9 us
    all_to_all x1, starting transfers between devices, regroup_tokens(): lax.all_to_all(signal, 'seq', split_axis=1, concat_axis=1, tiled=True)  24 us
    all_gather x1, blocking collectives, on_device(): block_taps = lax.all_gather(filter_taps, 'chan', axis=1, tiled=True)  20.4 us
    all_to_all x1, starting transfers between devices, regroup_spectrum(): lax.all_to_all(jnp.concatenate([part_real, part_imag], axis=0), 'seq', sp...  9 us
  transfers between devices with their start and end apart: 2, of which 2 were waited for; matrix products, arithmetic and copies ran while one was open for 0% of the time, Pallas kernels for 0%

profile of v2, /device:TPU:16, one launch (start us, length us, event | category | flops | bytes accessed | tf_op | source)
XLA Modules:
  0.0 222.7 jit_solution(7192462512721058775)
XLA Ops:
  0.6 20.4 %all_gather.3 = f32[4,8192]{1,0:T(4,128)S(1)} all-gather(f32[4,512]{1,0:T(4,128)} %param.8), channel_id=1, replica_groups=mesh['seq'=64,'chan'=16] {'chan'}, dimensions={1}, use_global_device_ids=true | all-gather | bytes 139264 | tf_op jit(solution)/shard_map/all_gather | solution.py:145
  21.1 1.0 mul.504
  22.4 1.0 copy.29
  23.4 24.0 %all-to-all-start = ((f32[12,64,128]{2,0,1:T(8,128)}), f32[12,64,128]{2,0,1:T(8,128)S(1)}, u32[]{:S(2)}, u32[]{:S(2)}) async-start(f32[12,64,128]{2,0,1:T(8,128)} %copy.29), calls=%async_computation | async-start | bytes 1048576 | tf_op jit(solution)/shard_map/all_to_all | solution.py:27
  47.6 32.1 %all-to-all-done = f32[12,64,128]{2,0,1:T(8,128)S(1)} async-done(((f32[12,64,128]{2,0,1:T(8,128)}), f32[12,64,128]{2,0,1:T(8,128)S(1)}, u32[]{:S(2)}, u32[]{:S(2)}) %all-to-all-start) | async-done | bytes 393248 | tf_op jit(solution)/shard_map/all_to_all | solution.py:27
  81.2 1.3 copy.32
  82.5 9.0 %all-to-all-start.1 = ((f32[24,64,128]{2,0,1:T(8,128)}), f32[24,64,128]{2,0,1:T(8,128)S(1)}, u32[]{:S(2)}, u32[]{:S(2)}) async-start(f32[24,64,128]{2,0,1:T(8,128)} %copy.32), calls=%async_computation.1 | async-start | bytes 1572864 | tf_op jit(solution)/shard_map/all_to_all | solution.py:32
  92.3 41.6 %all-to-all-done.1 = f32[24,64,128]{2,0,1:T(8,128)S(1)} async-done(((f32[24,64,128]{2,0,1:T(8,128)}), f32[24,64,128]{2,0,1:T(8,128)S(1)}, u32[]{:S(2)}, u32[]{:S(2)}) %all-to-all-start.1) | async-done | bytes 786464 | tf_op jit(solution)/shard_map/all_to_all | solution.py:32
  134.3 0.9 fusion.9
  135.2 0.9 fusion.6
  136.2 0.9 fusion.1
  137.1 0.9 fusion
  138.1 1.0 fusion.24
  139.1 1.0 fusion.25
  140.1 1.0 convolution_subtract_fusion
  141.2 1.0 convolution_add_fusion
  142.4 0.8 fusion.13
  143.2 0.8 fusion.14
  144.0 0.8 convolution_subtract_fusion.3
  144.9 1.1 multiply_subtract_fusion.1
  147.4 0.7 fusion.2
  149.4 40.2 %all_to_all.20 = f32[16,64,128]{2,0,1:T(8,128)S(1)} all-to-all(f32[16,64,128]{2,0,1:T(8,128)S(1)} %copy.40), channel_id=1, replica_groups=mesh['seq'=64,'chan'=16] {'seq'}, dimensions={1} | all-to-all | bytes 1048576 | tf_op jit(solution)/shard_map/all_to_all | solution.py:32
  190.9 30.9 %all_to_all.21 = f32[8,64,128]{2,0,1:T(8,128)S(1)} all-to-all(f32[8,64,128]{2,0,1:T(8,128)S(1)} %copy.43), channel_id=1, replica_groups=mesh['seq'=64,'chan'=16] {'seq'}, dimensions={1} | all-to-all | bytes 524288 | tf_op jit(solution)/shard_map/all_to_all | solution.py:27
  221.9 0.8 fusion.27
  (37 shorter events, 7.2 us)
Async XLA Ops:
  0.6 20.4 %copy-start = (f32[4,8192]{1,0:T(4,128)S(1)}, f32[4,8192]{1,0:T(4,128)}, u32[]{:S(2)}) copy-start(f32[4,8192]{1,0:T(4,128)} %param.6) | copy-start | bytes 393220
  21.1 1.0 copy-start.1
  21.1 1.0 copy-start.3
  23.4 56.3 %all-to-all-start = ((f32[12,64,128]{2,0,1:T(8,128)}), f32[12,64,128]{2,0,1:T(8,128)S(1)}, u32[]{:S(2)}, u32[]{:S(2)}) async-start(f32[12,64,128]{2,0,1:T(8,128)} %copy.29), calls=%async_computation | async-start | bytes 1048576 | tf_op jit(solution)/shard_map/all_to_all | solution.py:27
  82.5 51.4 %all-to-all-start.1 = ((f32[24,64,128]{2,0,1:T(8,128)}), f32[24,64,128]{2,0,1:T(8,128)S(1)}, u32[]{:S(2)}, u32[]{:S(2)}) async-start(f32[24,64,128]{2,0,1:T(8,128)} %copy.32), calls=%async_computation.1 | async-start | bytes 1572864 | tf_op jit(solution)/shard_map/all_to_all | solution.py:32
  190.9 31.0 %copy-start.2 = (f32[4,8192]{1,0:T(4,128)S(1)}, f32[4,8192]{1,0:T(4,128)}, u32[]{:S(2)}) copy-start(f32[4,8192]{1,0:T(4,128)} %param.7) | copy-start | bytes 393220

commit v3 on v2

--- a/solution.py
+++ b/solution.py
@@ -79,6 +79,23 @@
 def alternating(count, axis):
     index = lax.broadcasted_iota(jnp.int32, (count, count), axis)
     return (1 - 2 * (index % 2)).astype(jnp.float32)
+
+
+def split_columns(moved_real, moved_imag, rank, blocks, width, tokens):
+    period = 2 * blocks * tokens
+    lead = rank == 0
+    edge_real, edge_imag = column_twist(blocks, blocks, width, period, -1.0)
+    low_real = moved_real
+    low_imag = jnp.where(lead, 0.0, moved_imag)
+    high_real = jnp.where(lead, moved_imag * edge_real, 0.0)
+    high_imag = jnp.where(lead, moved_imag * edge_imag, 0.0)
+    return finish_forward(
+        jnp.stack([low_real, high_real], axis=2),
+        jnp.stack([low_imag, high_imag], axis=2),
+        blocks,
+        width,
+        tokens,
+    )
 
 
 def forward_spectrum(signal):
@@ -102,15 +119,31 @@
         mixed_real * turn_real - mixed_imag * turn_imag,
         mixed_real * turn_imag + mixed_imag * turn_real,
     )
-    lead = rank == 0
-    edge_real, edge_imag = column_twist(blocks, blocks, width, period, -1.0)
-    low_real = moved_real
-    low_imag = jnp.where(lead, 0.0, moved_imag)
-    high_real = jnp.where(lead, moved_imag * edge_real, 0.0)
-    high_imag = jnp.where(lead, moved_imag * edge_imag, 0.0)
-    return finish_forward(
-        jnp.stack([low_real, high_real], axis=2),
-        jnp.stack([low_imag, high_imag], axis=2),
+    return split_columns(moved_real, moved_imag, rank, blocks, width, tokens)
+
+
+def filter_spectrum(taps, tokens):
+    filters, piece = taps.shape
+    blocks = lax.axis_size("seq")
+    width = tokens // blocks
+    freqs = 2 * blocks
+    period = freqs * tokens
+    rank = lax.axis_index("seq")
+    column = lax.broadcasted_iota(jnp.int32, (blocks,), 0)
+    angles = (rank * column % freqs).astype(jnp.float32) * (-2.0 * math.pi / freqs)
+    weight_real = jnp.where(column == 0, 1.0, jnp.cos(angles))
+    weight_imag = jnp.where(column == 0, (1 - 2 * (rank % 2)).astype(jnp.float32), jnp.sin(angles))
+    parts = jnp.concatenate(
+        [weight_real[:, None, None] * taps[None], weight_imag[:, None, None] * taps[None]], axis=1
+    )
+    summed = lax.psum_scatter(parts, "seq", scatter_dimension=0, tiled=True)
+    full = lax.all_gather(summed, "chan", axis=2, tiled=True).reshape(2 * filters, blocks, width)
+    own_real, own_imag = column_twist(rank, blocks, width, period, -1.0)
+    base_real, base_imag = full[:filters], full[filters:]
+    return split_columns(
+        base_real * own_real - base_imag * own_imag,
+        base_real * own_imag + base_imag * own_real,
+        rank,
         blocks,
         width,
         tokens,
@@ -142,20 +175,14 @@
 
 
 def on_device(query_gate, key_gate, value_input, filter_taps, cotangent):
-    block_taps = lax.all_gather(filter_taps, "chan", axis=1, tiled=True)
     gated = key_gate * value_input
     weighted = cotangent * query_gate
-    rows = gated.shape[0]
-    filters = block_taps.shape[0]
-    all_real, all_imag = forward_spectrum(
-        jnp.concatenate([block_taps, gated, weighted], axis=0)
-    )
-    filter_real, filter_imag = all_real[:filters], all_imag[:filters]
-    gated_real = all_real[filters:filters + rows]
-    gated_imag = all_imag[filters:filters + rows]
-    weighted_real = all_real[filters + rows:]
-    weighted_imag = all_imag[filters + rows:]
-    reps = rows // filters
+    rows, tokens = gated.shape
+    filter_real, filter_imag = filter_spectrum(filter_taps, tokens)
+    all_real, all_imag = forward_spectrum(jnp.concatenate([gated, weighted], axis=0))
+    gated_real, gated_imag = all_real[:rows], all_imag[:rows]
+    weighted_real, weighted_imag = all_real[rows:], all_imag[rows:]
+    reps = rows // filter_real.shape[0]
     filter_real = jnp.tile(filter_real, (reps, 1, 1, 1))
     filter_imag = jnp.tile(filter_imag, (reps, 1, 1, 1))
     both = inverse_spectrum(

time: 223 us -> 856 us (3.84)
  waiting for transfers between devices: 73.7 us -> 685 us
  between operations: 0.99 us -> 14.4 us
    reduce_scatter x0 -> x1, waiting for transfers between devices: none -> 664 us  [filter_spectrum(): summed = lax.psum_scatter(parts, 'seq', scatter_dimension=0, tiled=True)]
    all_to_all x1, waiting for transfers between devices: 41.6 us -> 0.01 us  [regroup_spectrum(): lax.all_to_all(jnp.concatenate([part_real, part_imag], axis=0), 'seq', sp...]
    all_to_all x1, waiting for transfers between devices: 32.1 us -> 21.2 us  [regroup_tokens(): lax.all_to_all(signal, 'seq', split_axis=1, concat_axis=1, tiled=True)]
  transfers between devices with their start and end apart: 2 -> 3, of which waited for: 2 -> 2; matrix products, arithmetic and copies ran while one was open for 0% -> 1% of each run, Pallas kernels for 0% -> 0%
where the time goes in v3:
time: 856 us; the launch traced here: 855 us
  waiting for transfers between devices  685 us (80%)
  blocking collectives  95.6 us (11%)
  starting transfers between devices  32.1 us (4%)
  matrix products  19.5 us (2%)
  between operations  14.4 us (2%)
    reduce_scatter x1, waiting for transfers between devices, filter_spectrum(): summed = lax.psum_scatter(parts, 'seq', scatter_dimension=0, tiled=True)  664 us
    all_to_all x1, blocking collectives, regroup_spectrum(): lax.all_to_all(jnp.concatenate([part_real, part_imag], axis=0), 'seq', sp...  45.3 us
    all_to_all x1, blocking collectives, regroup_tokens(): lax.all_to_all(signal, 'seq', split_axis=1, concat_axis=1, tiled=True)  30.5 us
    all_to_all x1, starting transfers between devices, regroup_tokens(): lax.all_to_all(signal, 'seq', split_axis=1, concat_axis=1, tiled=True)  24.9 us
    all_to_all x1, waiting for transfers between devices, regroup_tokens(): lax.all_to_all(signal, 'seq', split_axis=1, concat_axis=1, tiled=True)  21.2 us
    all_gather x1, blocking collectives, filter_spectrum(): lax.all_gather(summed, 'chan', axis=2, tiled=True)  19.7 us
  transfers between devices with their start and end apart: 3, of which 2 were waited for; matrix products, arithmetic and copies ran while one was open for 1% of the time, Pallas kernels for 0%

profile of v3, /device:TPU:16, one launch (start us, length us, event | category | flops | bytes accessed | tf_op | source)
XLA Modules:
  0.0 855.3 jit_solution(2389469144542787808)
XLA Ops:
  8.1 1.2 pad_maximum_fusion
  9.4 0.9 copy-done.1
  10.4 0.9 copy-done
  11.3 0.8 maximum_bitcast_fusion
  12.1 24.9 %all-to-all-start = ((f32[8,64,128]{2,0,1:T(8,128)}), f32[8,64,128]{2,0,1:T(8,128)S(1)}, u32[]{:S(2)}, u32[]{:S(2)}) async-start(f32[8,64,128]{2,0,1:T(8,128)} %maximum_bitcast_fusion), calls=%async_computation | async-start | bytes 524288 | tf_op jit(solution)/shard_map/all_to_all | solution.py:27
  38.1 21.2 %all-to-all-done = f32[8,64,128]{2,0,1:T(8,128)S(1)} async-done(((f32[8,64,128]{2,0,1:T(8,128)}), f32[8,64,128]{2,0,1:T(8,128)S(1)}, u32[]{:S(2)}, u32[]{:S(2)}) %all-to-all-start) | async-done | bytes 262176 | tf_op jit(solution)/shard_map/all_to_all | solution.py:27
  60.5 1.1 copy.18
  61.6 7.2 all-to-all-start.1
  68.8 663.7 %reduce-scatter.2.cloned.1.call-done = f32[1,8,512]{2,1,0:T(8,128)} async-done(((f32[64,8,512]{2,1,0:T(8,128)}), f32[1,8,512]{2,1,0:T(8,128)}) %reduce-scatter.2.cloned.1.call-update) | async-done | bytes 16400 | tf_op jit(solution)/shard_map/reduce_scatter | solution.py:139
  732.5 19.7 %all_gather.3 = f32[1,8,8192]{2,1,0:T(8,128)S(1)} all-gather(f32[1,8,512]{2,1,0:T(8,128)} %reduce-scatter.2.cloned.1.call-done), channel_id=1, replica_groups=mesh['seq'=64,'chan'=16] {'chan'}, dimensions={2}, use_global_device_ids=true | all-gather | bytes 278528 | tf_op jit(solution)/shard_map/all_gather | solution.py:140
  758.7 0.7 fusion.3
  759.5 0.8 fusion.32
  760.3 0.8 fusion.31
  761.1 0.8 convolution_add_fusion.2
  762.0 0.8 convolution_subtract_fusion.2
  763.5 0.8 fusion.18
  764.3 1.0 fusion.17
  765.4 0.8 convolution_subtract_fusion.1
  766.2 0.9 multiply_subtract_fusion
  768.5 0.7 fusion.1
  769.3 0.7 fusion
  770.5 45.3 %all_to_all.20 = f32[16,64,128]{2,0,1:T(8,128)S(1)} all-to-all(f32[16,64,128]{2,0,1:T(8,128)S(1)} %copy.27), channel_id=1, replica_groups=mesh['seq'=64,'chan'=16] {'seq'}, dimensions={1} | all-to-all | bytes 1048576 | tf_op jit(solution)/shard_map/all_to_all | solution.py:32
  817.1 30.5 %all_to_all.21 = f32[8,64,128]{2,0,1:T(8,128)S(1)} all-to-all(f32[8,64,128]{2,0,1:T(8,128)S(1)} %copy.30), channel_id=1, replica_groups=mesh['seq'=64,'chan'=16] {'seq'}, dimensions={1} | all-to-all | bytes 524288 | tf_op jit(solution)/shard_map/all_to_all | solution.py:27
  847.7 0.8 fusion.36
  (52 shorter events, 13.6 us)
Async XLA Ops:
  7.2 725.3 %reduce-scatter.2.cloned.1.call-start = ((), (), s32[]{:S(2)}) async-start(), calls=%async_computation.5 | async-start | bytes 1064960 | tf_op jit(solution)/shard_map/reduce_scatter | solution.py:139
  7.2 0.7 copy-start.4
  9.4 0.9 copy-start.1
  9.4 1.0 copy-start.3
  10.3 0.9 copy-start
  10.3 1.0 copy-start.2
  12.1 47.3 %all-to-all-start = ((f32[8,64,128]{2,0,1:T(8,128)}), f32[8,64,128]{2,0,1:T(8,128)S(1)}, u32[]{:S(2)}, u32[]{:S(2)}) async-start(f32[8,64,128]{2,0,1:T(8,128)} %maximum_bitcast_fusion), calls=%async_computation | async-start | bytes 524288 | tf_op jit(solution)/shard_map/all_to_all | solution.py:27
  61.6 694.7 %all-to-all-start.1 = ((f32[16,64,128]{2,0,1:T(8,128)}), f32[16,64,128]{2,0,1:T(8,128)S(1)}, u32[]{:S(2)}, u32[]{:S(2)}) async-start(f32[16,64,128]{2,0,1:T(8,128)} %copy.18), calls=%async_computation.1 | async-start | bytes 1048576 | tf_op jit(solution)/shard_map/all_to_all | solution.py:32
Sparse Core Ops, SparseCore 0:
  13.5 718.8 reduce-scatter.1

commit v4 on v2

--- a/solution.py
+++ b/solution.py
@@ -102,22 +102,10 @@
         mixed_real * turn_real - mixed_imag * turn_imag,
         mixed_real * turn_imag + mixed_imag * turn_real,
     )
-    lead = rank == 0
-    edge_real, edge_imag = column_twist(blocks, blocks, width, period, -1.0)
-    low_real = moved_real
-    low_imag = jnp.where(lead, 0.0, moved_imag)
-    high_real = jnp.where(lead, moved_imag * edge_real, 0.0)
-    high_imag = jnp.where(lead, moved_imag * edge_imag, 0.0)
-    return finish_forward(
-        jnp.stack([low_real, high_real], axis=2),
-        jnp.stack([low_imag, high_imag], axis=2),
-        blocks,
-        width,
-        tokens,
-    )
-
-
-def inverse_spectrum(spectrum_real, spectrum_imag):
+    return moved_real, moved_imag
+
+
+def inverse_spectrum(spectrum_real, spectrum_imag, high_real):
     count, blocks, per_device, width = spectrum_real.shape
     tokens = blocks * width
     freqs = 2 * blocks
@@ -125,10 +113,8 @@
     rank = lax.axis_index("seq")
     spread_real, spread_imag = start_inverse(spectrum_real, spectrum_imag, blocks, width, tokens)
     own_real, own_imag = column_twist(rank, blocks, width, period, 1.0)
-    edge_real, edge_imag = column_twist(blocks, blocks, width, period, 1.0)
     low_real = spread_real[:, :, 0] * own_real - spread_imag[:, :, 0] * own_imag
     low_imag = spread_real[:, :, 0] * own_imag + spread_imag[:, :, 0] * own_real
-    high_real = spread_real[:, :, 1] * edge_real - spread_imag[:, :, 1] * edge_imag
     moved_real, moved_imag = regroup_spectrum(
         low_real, jnp.where(rank == 0, high_real, low_imag)
     )
@@ -141,15 +127,7 @@
     return regroup_tokens(rebuilt).reshape(count, tokens)
 
 
-def on_device(query_gate, key_gate, value_input, filter_taps, cotangent):
-    block_taps = lax.all_gather(filter_taps, "chan", axis=1, tiled=True)
-    gated = key_gate * value_input
-    weighted = cotangent * query_gate
-    rows = gated.shape[0]
-    filters = block_taps.shape[0]
-    all_real, all_imag = forward_spectrum(
-        jnp.concatenate([block_taps, gated, weighted], axis=0)
-    )
+def spectral_products(all_real, all_imag, filters, rows):
     filter_real, filter_imag = all_real[:filters], all_imag[:filters]
     gated_real = all_real[filters:filters + rows]
     gated_imag = all_imag[filters:filters + rows]
@@ -158,22 +136,64 @@
     reps = rows // filters
     filter_real = jnp.tile(filter_real, (reps, 1, 1, 1))
     filter_imag = jnp.tile(filter_imag, (reps, 1, 1, 1))
-    both = inverse_spectrum(
-        jnp.concatenate(
-            [
-                gated_real * filter_real - gated_imag * filter_imag,
-                weighted_real * filter_real + weighted_imag * filter_imag,
-            ],
-            axis=0,
-        ),
-        jnp.concatenate(
-            [
-                gated_real * filter_imag + gated_imag * filter_real,
-                weighted_imag * filter_real - weighted_real * filter_imag,
-            ],
-            axis=0,
-        ),
-    )
+    product_real = jnp.concatenate(
+        [
+            gated_real * filter_real - gated_imag * filter_imag,
+            weighted_real * filter_real + weighted_imag * filter_imag,
+        ],
+        axis=0,
+    )
+    product_imag = jnp.concatenate(
+        [
+            gated_real * filter_imag + gated_imag * filter_real,
+            weighted_imag * filter_real - weighted_real * filter_imag,
+        ],
+        axis=0,
+    )
+    return product_real, product_imag
+
+
+def on_device(query_gate, key_gate, value_input, filter_taps, cotangent):
+    block_taps = lax.all_gather(filter_taps, "chan", axis=1, tiled=True)
+    gated = key_gate * value_input
+    weighted = cotangent * query_gate
+    rows, tokens = gated.shape
+    filters = block_taps.shape[0]
+    blocks = lax.axis_size("seq")
+    width = tokens // blocks
+    period = 2 * blocks * tokens
+    rank = lax.axis_index("seq")
+    lead = rank == 0
+    moved_real, moved_imag = forward_spectrum(
+        jnp.concatenate([block_taps, gated, weighted], axis=0)
+    )
+    low_real, low_imag = finish_forward(
+        moved_real[:, :, None],
+        jnp.where(lead, 0.0, moved_imag)[:, :, None],
+        blocks,
+        width,
+        tokens,
+    )
+
+    def edge_column():
+        edge_real, edge_imag = column_twist(blocks, blocks, width, period, -1.0)
+        high_real, high_imag = finish_forward(
+            (moved_imag * edge_real)[:, :, None],
+            (moved_imag * edge_imag)[:, :, None],
+            blocks,
+            width,
+            tokens,
+        )
+        spread_real, spread_imag = start_inverse(
+            *spectral_products(high_real, high_imag, filters, rows), blocks, width, tokens
+        )
+        back_real, back_imag = column_twist(blocks, blocks, width, period, 1.0)
+        return spread_real[:, :, 0] * back_real - spread_imag[:, :, 0] * back_imag
+
+    high = lax.cond(
+        lead, edge_column, lambda: jnp.zeros((2 * rows, blocks, width), jnp.float32)
+    )
+    both = inverse_spectrum(*spectral_products(low_real, low_imag, filters, rows), high)
     convolved = both[:rows]
     gated_grad = both[rows:]
     return (cotangent * convolved, gated_grad * value_input, gated_grad * key_gate)

time: 223 us -> 221 us (level)
  the two profiles are of different devices: /device:TPU:16 before, /device:TPU:8 now
where the time goes in v4:
time: 221 us; the launch traced here: 220 us
  blocking collectives  87.8 us (40%)
  waiting for transfers between devices  74.2 us (34%)
  starting transfers between devices  27.6 us (12%)
  matrix products  22.7 us (10%)
  other arithmetic  3.45 us (2%)
  local copies, waits for them, and re-layouts  3.26 us (1%)
    all_to_all x1, waiting for transfers between devices, regroup_spectrum(): lax.all_to_all(jnp.concatenate([part_real, part_imag], axis=0), 'seq', sp...  42 us
    all_to_all x1, blocking collectives, regroup_spectrum(): lax.all_to_all(jnp.concatenate([part_real, part_imag], axis=0), 'seq', sp...  33.2 us
    all_to_all x1, waiting for transfers between devices, regroup_tokens(): lax.all_to_all(signal, 'seq', split_axis=1, concat_axis=1, tiled=True)  32.2 us
    all_to_all x1, blocking collectives, regroup_tokens(): lax.all_to_all(signal, 'seq', split_axis=1, concat_axis=1, tiled=True)  29 us
    all_gather x1, blocking collectives, on_device(): block_taps = lax.all_gather(filter_taps, 'chan', axis=1, tiled=True)  25.6 us
    all_to_all x1, starting transfers between devices, regroup_tokens(): lax.all_to_all(signal, 'seq', split_axis=1, concat_axis=1, tiled=True)  18.7 us
    all_to_all x1, starting transfers between devices, regroup_spectrum(): lax.all_to_all(jnp.concatenate([part_real, part_imag], axis=0), 'seq', sp...  8.87 us
    dot_general x8, matrix products, complex_mix(): product(table_imag, data_real)  5.14 us
  transfers between devices with their start and end apart: 2, of which 2 were waited for; matrix products, arithmetic and copies ran while one was open for 0% of the time, Pallas kernels for 0%

profile of v4, /device:TPU:8, one launch (start us, length us, event | category | flops | bytes accessed | tf_op | source)
XLA Modules:
  0.0 220.4 jit_solution(11700855275169958528)
XLA Ops:
  0.6 25.6 %all_gather.3 = f32[4,8192]{1,0:T(4,128)S(1)} all-gather(f32[4,512]{1,0:T(4,128)} %param.10), channel_id=1, replica_groups=mesh['seq'=64,'chan'=16] {'chan'}, dimensions={1}, use_global_device_ids=true | all-gather | bytes 139264 | tf_op jit(solution)/shard_map/all_gather | solution.py:157
  26.3 1.0 mul.735
  27.6 1.0 copy.17
  28.6 18.7 %all-to-all-start = ((f32[12,64,128]{2,0,1:T(8,128)}), f32[12,64,128]{2,0,1:T(8,128)S(1)}, u32[]{:S(2)}, u32[]{:S(2)}) async-start(f32[12,64,128]{2,0,1:T(8,128)} %copy.17), calls=%async_computation | async-start | bytes 1048576 | tf_op jit(solution)/shard_map/all_to_all | solution.py:27
  47.5 32.2 %all-to-all-done = f32[12,64,128]{2,0,1:T(8,128)S(1)} async-done(((f32[12,64,128]{2,0,1:T(8,128)}), f32[12,64,128]{2,0,1:T(8,128)S(1)}, u32[]{:S(2)}, u32[]{:S(2)}) %all-to-all-start) | async-done | bytes 393248 | tf_op jit(solution)/shard_map/all_to_all | solution.py:27
  79.7 0.7 convolution_bitcast_fusion.1
  80.4 0.7 multiply_subtract_fusion.7
  81.2 1.3 copy.20
  82.5 8.9 %all-to-all-start.1 = ((f32[24,64,128]{2,0,1:T(8,128)}), f32[24,64,128]{2,0,1:T(8,128)S(1)}, u32[]{:S(2)}, u32[]{:S(2)}) async-start(f32[24,64,128]{2,0,1:T(8,128)} %copy.20), calls=%async_computation.1 | async-start | bytes 1572864 | tf_op jit(solution)/shard_map/all_to_all | solution.py:32
  92.0 42.0 %all-to-all-done.1 = f32[24,64,128]{2,0,1:T(8,128)S(1)} async-done(((f32[24,64,128]{2,0,1:T(8,128)}), f32[24,64,128]{2,0,1:T(8,128)S(1)}, u32[]{:S(2)}, u32[]{:S(2)}) %all-to-all-start.1) | async-done | bytes 786464 | tf_op jit(solution)/shard_map/all_to_all | solution.py:32
  134.8 0.7 fusion.176
  135.5 0.7 fusion.160
  136.8 0.7 fusion.166
  137.6 0.7 fusion.170
  138.3 0.7 convolution_add_fusion.4
  139.0 0.7 convolution_subtract_fusion.4
  144.0 11.2 %conditional.1 = (f32[8,64,128]{2,1,0:T(8,128)S(1)}) conditional(s32[]{:T(128)} %convert_element_type.203, () %tuple.14, f32[12,64,128]{2,1,0:T(8,128)S(1)} %copy.28), branch_computations={%region_0.1_spmd, %region_1.2_spmd} | conditional | flops 1516470272 | bytes 18285064 | solution.py:193
  147.4 0.7 fusion.7
  148.1 0.7 convolution_add_fusion
  148.9 0.7 fusion.11
  149.6 0.7 convolution_subtract_fusion
  156.1 33.2 %all_to_all.20 = f32[16,64,128]{2,0,1:T(8,128)S(1)} all-to-all(f32[16,64,128]{2,0,1:T(8,128)S(1)} %copy.23), channel_id=1, replica_groups=mesh['seq'=64,'chan'=16] {'seq'}, dimensions={1} | all-to-all | bytes 1048576 | tf_op jit(solution)/shard_map/all_to_all | solution.py:32
  190.6 29.0 %all_to_all.21 = f32[8,64,128]{2,0,1:T(8,128)S(1)} all-to-all(f32[8,64,128]{2,0,1:T(8,128)S(1)} %copy.26), channel_id=1, replica_groups=mesh['seq'=64,'chan'=16] {'seq'}, dimensions={1} | all-to-all | bytes 524288 | tf_op jit(solution)/shard_map/all_to_all | solution.py:27
  219.6 0.8 fusion.190
  (55 shorter events, 16.8 us)
Async XLA Ops:
  0.6 25.6 %copy-start.1 = (f32[4,8192]{1,0:T(4,128)S(1)}, f32[4,8192]{1,0:T(4,128)}, u32[]{:S(2)}) copy-start(f32[4,8192]{1,0:T(4,128)} %param.11) | copy-start | bytes 393220
  26.3 1.0 copy-start
  26.3 1.0 copy-start.2
  28.6 51.1 %all-to-all-start = ((f32[12,64,128]{2,0,1:T(8,128)}), f32[12,64,128]{2,0,1:T(8,128)S(1)}, u32[]{:S(2)}, u32[]{:S(2)}) async-start(f32[12,64,128]{2,0,1:T(8,128)} %copy.17), calls=%async_computation | async-start | bytes 1048576 | tf_op jit(solution)/shard_map/all_to_all | solution.py:27
  82.5 51.4 %all-to-all-start.1 = ((f32[24,64,128]{2,0,1:T(8,128)}), f32[24,64,128]{2,0,1:T(8,128)S(1)}, u32[]{:S(2)}, u32[]{:S(2)}) async-start(f32[24,64,128]{2,0,1:T(8,128)} %copy.20), calls=%async_computation.1 | async-start | bytes 1572864 | tf_op jit(solution)/shard_map/all_to_all | solution.py:32

commit v5 on v4

--- a/solution.py
+++ b/solution.py
@@ -154,7 +154,11 @@
 
 
 def on_device(query_gate, key_gate, value_input, filter_taps, cotangent):
-    block_taps = lax.all_gather(filter_taps, "chan", axis=1, tiled=True)
+    peers = lax.axis_size("chan")
+    copies = jnp.broadcast_to(filter_taps[None], (peers,) + filter_taps.shape)
+    block_taps = jnp.moveaxis(
+        lax.all_to_all(copies, "chan", split_axis=0, concat_axis=0, tiled=True), 0, 1
+    ).reshape(filter_taps.shape[0], peers * filter_taps.shape[1])
     gated = key_gate * value_input
     weighted = cotangent * query_gate
     rows, tokens = gated.shape

time: 221 us -> 212 us (0.959)
  the two profiles are of different devices: /device:TPU:8 before, /device:TPU:16 now
where the time goes in v5:
time: 212 us; the launch traced here: 211 us
  waiting for transfers between devices  79.2 us (37%)
  blocking collectives  72.8 us (34%)
  starting transfers between devices  38.5 us (18%)
  matrix products  12.7 us (6%)
  other arithmetic  3.53 us (2%)
  local copies, waits for them, and re-layouts  3.47 us (2%)
    all_to_all x1, blocking collectives, regroup_spectrum(): lax.all_to_all(jnp.concatenate([part_real, part_imag], axis=0), 'seq', sp...  43.5 us
    all_to_all x1, waiting for transfers between devices, regroup_spectrum(): lax.all_to_all(jnp.concatenate([part_real, part_imag], axis=0), 'seq', sp...  42 us
    all_to_all x1, waiting for transfers between devices, regroup_tokens(): lax.all_to_all(signal, 'seq', split_axis=1, concat_axis=1, tiled=True)  31.5 us
    all_to_all x1, blocking collectives, regroup_tokens(): lax.all_to_all(signal, 'seq', split_axis=1, concat_axis=1, tiled=True)  29.3 us
    all_to_all x1, starting transfers between devices, regroup_tokens(): lax.all_to_all(signal, 'seq', split_axis=1, concat_axis=1, tiled=True)  24 us
    all_to_all x1, starting transfers between devices, regroup_spectrum(): lax.all_to_all(jnp.concatenate([part_real, part_imag], axis=0), 'seq', sp...  8.91 us
    all_to_all x1, waiting for transfers between devices, on_device(): lax.all_to_all(copies, 'chan', split_axis=0, concat_axis=0, tiled=True)  5.69 us
    all_to_all x1, starting transfers between devices, on_device(): lax.all_to_all(copies, 'chan', split_axis=0, concat_axis=0, tiled=True)  5.55 us
  transfers between devices with their start and end apart: 3, of which 3 were waited for; matrix products, arithmetic and copies ran while one was open for 1% of the time, Pallas kernels for 0%

profile of v5, /device:TPU:16, one launch (start us, length us, event | category | flops | bytes accessed | tf_op | source)
XLA Modules:
  0.0 211.4 jit_solution(17777566892473665309)
XLA Ops:
  0.6 1.4 broadcast_in_dim.10
  2.0 5.5 %all-to-all-start = ((f32[16,4,512]{2,1,0:T(4,128)}), f32[16,4,512]{2,1,0:T(4,128)S(1)}, u32[]{:S(2)}, u32[]{:S(2)}) async-start(f32[16,4,512]{2,1,0:T(4,128)} %broadcast_in_dim.10), calls=%async_computation | async-start | bytes 262144 | tf_op jit(solution)/shard_map/all_to_all | solution.py:160
  7.6 1.0 multiply_bitcast_fusion
  8.6 5.7 %all-to-all-done = f32[16,4,512]{2,1,0:T(4,128)S(1)} async-done(((f32[16,4,512]{2,1,0:T(4,128)}), f32[16,4,512]{2,1,0:T(4,128)S(1)}, u32[]{:S(2)}, u32[]{:S(2)}) %all-to-all-start) | async-done | bytes 131104 | tf_op jit(solution)/shard_map/all_to_all | solution.py:160
  14.3 0.9 pad_maximum_fusion.1
  15.2 24.0 %all-to-all-start.1 = ((f32[12,64,128]{2,0,1:T(8,128)}), f32[12,64,128]{2,0,1:T(8,128)S(1)}, u32[]{:S(2)}, u32[]{:S(2)}) async-start(f32[12,64,128]{2,0,1:T(8,128)} %pad_maximum_fusion.1), calls=%async_computation.1 | async-start | bytes 1048576 | tf_op jit(solution)/shard_map/all_to_all | solution.py:27
  39.4 31.5 %all-to-all-done.1 = f32[12,64,128]{2,0,1:T(8,128)S(1)} async-done(((f32[12,64,128]{2,0,1:T(8,128)}), f32[12,64,128]{2,0,1:T(8,128)S(1)}, u32[]{:S(2)}, u32[]{:S(2)}) %all-to-all-start.1) | async-done | bytes 393248 | tf_op jit(solution)/shard_map/all_to_all | solution.py:27
  70.9 0.7 convolution_bitcast_fusion.1
  71.6 0.7 multiply_subtract_fusion.7
  72.4 1.3 copy.10
  73.7 8.9 %all-to-all-start.2 = ((f32[24,64,128]{2,0,1:T(8,128)}), f32[24,64,128]{2,0,1:T(8,128)S(1)}, u32[]{:S(2)}, u32[]{:S(2)}) async-start(f32[24,64,128]{2,0,1:T(8,128)} %copy.10), calls=%async_computation.2 | async-start | bytes 1572864 | tf_op jit(solution)/shard_map/all_to_all | solution.py:32
  83.2 42.0 %all-to-all-done.2 = f32[24,64,128]{2,0,1:T(8,128)S(1)} async-done(((f32[24,64,128]{2,0,1:T(8,128)}), f32[24,64,128]{2,0,1:T(8,128)S(1)}, u32[]{:S(2)}, u32[]{:S(2)}) %all-to-all-start.2) | async-done | bytes 786464 | tf_op jit(solution)/shard_map/all_to_all | solution.py:32
  125.4 0.6 fusion.172
  126.1 0.7 fusion.176
  126.8 0.7 fusion.160
  127.4 0.6 fusion.161
  128.1 0.7 fusion.166
  128.8 0.7 fusion.170
  129.5 0.7 convolution_add_fusion.4
  130.3 0.7 convolution_subtract_fusion.4
  135.5 0.6 multiply_subtract_fusion.8
  136.5 43.5 %all_to_all.25 = f32[16,64,128]{2,0,1:T(8,128)S(1)} all-to-all(f32[16,64,128]{2,0,1:T(8,128)S(1)} %copy.13), channel_id=1, replica_groups=mesh['seq'=64,'chan'=16] {'seq'}, dimensions={1} | all-to-all | bytes 1048576 | tf_op jit(solution)/shard_map/all_to_all | solution.py:32
  181.3 29.3 %all_to_all.26 = f32[8,64,128]{2,0,1:T(8,128)S(1)} all-to-all(f32[8,64,128]{2,0,1:T(8,128)S(1)} %copy.16), channel_id=1, replica_groups=mesh['seq'=64,'chan'=16] {'seq'}, dimensions={1} | all-to-all | bytes 524288 | tf_op jit(solution)/shard_map/all_to_all | solution.py:27
  210.6 0.8 fusion.190
  (34 shorter events, 7.0 us)
Async XLA Ops:
  0.6 7.0 %copy-start.2 = (f32[4,8192]{1,0:T(4,128)S(1)}, f32[4,8192]{1,0:T(4,128)}, u32[]{:S(2)}) copy-start(f32[4,8192]{1,0:T(4,128)} %param.9) | copy-start | bytes 393220
  2.0 5.6 %copy-start = (f32[4,8192]{1,0:T(4,128)S(1)}, f32[4,8192]{1,0:T(4,128)}, u32[]{:S(2)}) copy-start(f32[4,8192]{1,0:T(4,128)} %param.8) | copy-start | bytes 393220
  2.0 5.6 %copy-start.1 = (f32[4,8192]{1,0:T(4,128)S(1)}, f32[4,8192]{1,0:T(4,128)}, u32[]{:S(2)}) copy-start(f32[4,8192]{1,0:T(4,128)} %param.11) | copy-start | bytes 393220
  2.0 12.3 %all-to-all-start = ((f32[16,4,512]{2,1,0:T(4,128)}), f32[16,4,512]{2,1,0:T(4,128)S(1)}, u32[]{:S(2)}, u32[]{:S(2)}) async-start(f32[16,4,512]{2,1,0:T(4,128)} %broadcast_in_dim.10), calls=%async_computation | async-start | bytes 262144 | tf_op jit(solution)/shard_map/all_to_all | solution.py:160
  15.2 55.7 %all-to-all-start.1 = ((f32[12,64,128]{2,0,1:T(8,128)}), f32[12,64,128]{2,0,1:T(8,128)S(1)}, u32[]{:S(2)}, u32[]{:S(2)}) async-start(f32[12,64,128]{2,0,1:T(8,128)} %pad_maximum_fusion.1), calls=%async_computation.1 | async-start | bytes 1048576 | tf_op jit(solution)/shard_map/all_to_all | solution.py:27
  73.7 51.5 %all-to-all-start.2 = ((f32[24,64,128]{2,0,1:T(8,128)}), f32[24,64,128]{2,0,1:T(8,128)S(1)}, u32[]{:S(2)}, u32[]{:S(2)}) async-start(f32[24,64,128]{2,0,1:T(8,128)} %copy.10), calls=%async_computation.2 | async-start | bytes 1572864 | tf_op jit(solution)/shard_map/all_to_all | solution.py:32

commit v6 on v2

--- a/solution.py
+++ b/solution.py
@@ -142,7 +142,11 @@
 
 
 def on_device(query_gate, key_gate, value_input, filter_taps, cotangent):
-    block_taps = lax.all_gather(filter_taps, "chan", axis=1, tiled=True)
+    peers = lax.axis_size("chan")
+    copies = jnp.broadcast_to(filter_taps[None], (peers,) + filter_taps.shape)
+    block_taps = jnp.moveaxis(
+        lax.all_to_all(copies, "chan", split_axis=0, concat_axis=0, tiled=True), 0, 1
+    ).reshape(filter_taps.shape[0], peers * filter_taps.shape[1])
     gated = key_gate * value_input
     weighted = cotangent * query_gate
     rows = gated.shape[0]

time: 223 us -> 214 us (0.960)
  blocking collectives: 91.5 us -> 71 us
  starting transfers between devices: 33 us -> 38.6 us
  waiting for transfers between devices: 73.7 us -> 78.8 us
    all_gather x1 -> x0, blocking collectives: 20.4 us -> none  [on_device(): block_taps = lax.all_gather(filter_taps, 'chan', axis=1, tiled=True)]
    all_to_all x0 -> x1, waiting for transfers between devices: none -> 5.69 us  [on_device(): lax.all_to_all(copies, 'chan', split_axis=0, concat_axis=0, tiled=True)]
    all_to_all x0 -> x1, starting transfers between devices: none -> 5.55 us  [on_device(): lax.all_to_all(copies, 'chan', split_axis=0, concat_axis=0, tiled=True)]
  transfers between devices with their start and end apart: 2 -> 3, of which waited for: 2 -> 3; matrix products, arithmetic and copies ran while one was open for 0% -> 1% of each run, Pallas kernels for 0% -> 0%
where the time goes in v6:
time: 214 us
  waiting for transfers between devices  78.8 us (37%)
  blocking collectives  71 us (33%)
  starting transfers between devices  38.6 us (18%)
  matrix products  16.8 us (8%)
  other arithmetic  4.2 us (2%)
  local copies, waits for them, and re-layouts  3.47 us (2%)
    all_to_all x1, waiting for transfers between devices, regroup_spectrum(): lax.all_to_all(jnp.concatenate([part_real, part_imag], axis=0), 'seq', sp...  41.6 us
    all_to_all x1, blocking collectives, regroup_spectrum(): lax.all_to_all(jnp.concatenate([part_real, part_imag], axis=0), 'seq', sp...  40.2 us
    all_to_all x1, waiting for transfers between devices, regroup_tokens(): lax.all_to_all(signal, 'seq', split_axis=1, concat_axis=1, tiled=True)  31.5 us
    all_to_all x1, blocking collectives, regroup_tokens(): lax.all_to_all(signal, 'seq', split_axis=1, concat_axis=1, tiled=True)  30.8 us
    all_to_all x1, starting transfers between devices, regroup_tokens(): lax.all_to_all(signal, 'seq', split_axis=1, concat_axis=1, tiled=True)  24 us
    all_to_all x1, starting transfers between devices, regroup_spectrum(): lax.all_to_all(jnp.concatenate([part_real, part_imag], axis=0), 'seq', sp...  9.07 us
    all_to_all x1, waiting for transfers between devices, on_device(): lax.all_to_all(copies, 'chan', split_axis=0, concat_axis=0, tiled=True)  5.69 us
    all_to_all x1, starting transfers between devices, on_device(): lax.all_to_all(copies, 'chan', split_axis=0, concat_axis=0, tiled=True)  5.55 us
  transfers between devices with their start and end apart: 3, of which 3 were waited for; matrix products, arithmetic and copies ran while one was open for 1% of the time, Pallas kernels for 0%

profile of v6, /device:TPU:16, one launch (start us, length us, event | category | flops | bytes accessed | tf_op | source)
XLA Modules:
  0.0 213.9 jit_solution(17894191822131573005)
XLA Ops:
  0.6 1.4 broadcast_in_dim.13
  2.0 5.5 %all-to-all-start = ((f32[16,4,512]{2,1,0:T(4,128)}), f32[16,4,512]{2,1,0:T(4,128)S(1)}, u32[]{:S(2)}, u32[]{:S(2)}) async-start(f32[16,4,512]{2,1,0:T(4,128)} %broadcast_in_dim.13), calls=%async_computation | async-start | bytes 262144 | tf_op jit(solution)/shard_map/all_to_all | solution.py:148
  7.6 1.0 multiply_bitcast_fusion
  8.6 5.7 %all-to-all-done = f32[16,4,512]{2,1,0:T(4,128)S(1)} async-done(((f32[16,4,512]{2,1,0:T(4,128)}), f32[16,4,512]{2,1,0:T(4,128)S(1)}, u32[]{:S(2)}, u32[]{:S(2)}) %all-to-all-start) | async-done | bytes 131104 | tf_op jit(solution)/shard_map/all_to_all | solution.py:148
  14.3 0.9 pad_maximum_fusion.5
  15.2 24.0 %all-to-all-start.1 = ((f32[12,64,128]{2,0,1:T(8,128)}), f32[12,64,128]{2,0,1:T(8,128)S(1)}, u32[]{:S(2)}, u32[]{:S(2)}) async-start(f32[12,64,128]{2,0,1:T(8,128)} %pad_maximum_fusion.5), calls=%async_computation.1 | async-start | bytes 1048576 | tf_op jit(solution)/shard_map/all_to_all | solution.py:27
  39.4 31.5 %all-to-all-done.1 = f32[12,64,128]{2,0,1:T(8,128)S(1)} async-done(((f32[12,64,128]{2,0,1:T(8,128)}), f32[12,64,128]{2,0,1:T(8,128)S(1)}, u32[]{:S(2)}, u32[]{:S(2)}) %all-to-all-start.1) | async-done | bytes 393248 | tf_op jit(solution)/shard_map/all_to_all | solution.py:27
  72.4 1.4 copy.17
  73.8 9.1 %all-to-all-start.2 = ((f32[24,64,128]{2,0,1:T(8,128)}), f32[24,64,128]{2,0,1:T(8,128)S(1)}, u32[]{:S(2)}, u32[]{:S(2)}) async-start(f32[24,64,128]{2,0,1:T(8,128)} %copy.17), calls=%async_computation.2 | async-start | bytes 1572864 | tf_op jit(solution)/shard_map/all_to_all | solution.py:32
  83.6 41.6 %all-to-all-done.2 = f32[24,64,128]{2,0,1:T(8,128)S(1)} async-done(((f32[24,64,128]{2,0,1:T(8,128)}), f32[24,64,128]{2,0,1:T(8,128)S(1)}, u32[]{:S(2)}, u32[]{:S(2)}) %all-to-all-start.2) | async-done | bytes 786464 | tf_op jit(solution)/shard_map/all_to_all | solution.py:32
  125.7 0.9 fusion.9
  126.6 0.9 fusion.6
  127.5 0.9 fusion.1
  128.5 0.9 fusion
  129.4 1.0 fusion.24
  130.5 1.0 fusion.25
  131.5 1.0 convolution_subtract_fusion
  132.5 1.0 convolution_add_fusion
  133.8 0.8 fusion.13
  135.4 0.8 convolution_subtract_fusion.3
  136.2 1.1 multiply_subtract_fusion.1
  140.8 40.2 %all_to_all.25 = f32[16,64,128]{2,0,1:T(8,128)S(1)} all-to-all(f32[16,64,128]{2,0,1:T(8,128)S(1)} %copy.25), channel_id=1, replica_groups=mesh['seq'=64,'chan'=16] {'seq'}, dimensions={1} | all-to-all | bytes 1048576 | tf_op jit(solution)/shard_map/all_to_all | solution.py:32
  182.2 30.8 %all_to_all.26 = f32[8,64,128]{2,0,1:T(8,128)S(1)} all-to-all(f32[8,64,128]{2,0,1:T(8,128)S(1)} %copy.28), channel_id=1, replica_groups=mesh['seq'=64,'chan'=16] {'seq'}, dimensions={1} | all-to-all | bytes 524288 | tf_op jit(solution)/shard_map/all_to_all | solution.py:27
  213.1 0.8 fusion.27
  (34 shorter events, 8.4 us)
Async XLA Ops:
  0.6 7.0 %copy-start.2 = (f32[4,8192]{1,0:T(4,128)S(1)}, f32[4,8192]{1,0:T(4,128)}, u32[]{:S(2)}) copy-start(f32[4,8192]{1,0:T(4,128)} %param.7) | copy-start | bytes 393220
  2.0 5.6 %copy-start = (f32[4,8192]{1,0:T(4,128)S(1)}, f32[4,8192]{1,0:T(4,128)}, u32[]{:S(2)}) copy-start(f32[4,8192]{1,0:T(4,128)} %param.6) | copy-start | bytes 393220
  2.0 5.6 %copy-start.1 = (f32[4,8192]{1,0:T(4,128)S(1)}, f32[4,8192]{1,0:T(4,128)}, u32[]{:S(2)}) copy-start(f32[4,8192]{1,0:T(4,128)} %param.9) | copy-start | bytes 393220
  2.0 12.3 %all-to-all-start = ((f32[16,4,512]{2,1,0:T(4,128)}), f32[16,4,512]{2,1,0:T(4,128)S(1)}, u32[]{:S(2)}, u32[]{:S(2)}) async-start(f32[16,4,512]{2,1,0:T(4,128)} %broadcast_in_dim.13), calls=%async_computation | async-start | bytes 262144 | tf_op jit(solution)/shard_map/all_to_all | solution.py:148
  15.2 55.7 %all-to-all-start.1 = ((f32[12,64,128]{2,0,1:T(8,128)}), f32[12,64,128]{2,0,1:T(8,128)S(1)}, u32[]{:S(2)}, u32[]{:S(2)}) async-start(f32[12,64,128]{2,0,1:T(8,128)} %pad_maximum_fusion.5), calls=%async_computation.1 | async-start | bytes 1048576 | tf_op jit(solution)/shard_map/all_to_all | solution.py:27
  73.8 51.5 %all-to-all-start.2 = ((f32[24,64,128]{2,0,1:T(8,128)}), f32[24,64,128]{2,0,1:T(8,128)S(1)}, u32[]{:S(2)}, u32[]{:S(2)}) async-start(f32[24,64,128]{2,0,1:T(8,128)} %copy.17), calls=%async_computation.2 | async-start | bytes 1572864 | tf_op jit(solution)/shard_map/all_to_all | solution.py:32

commit v7 on v5

--- a/solution.py
+++ b/solution.py
@@ -16,7 +16,7 @@
 
 
 def complex_mix(formula, table_real, table_imag, data_real, data_imag):
-    product = partial(jnp.einsum, formula, precision=lax.Precision.HIGHEST)
+    product = partial(jnp.einsum, formula, precision=lax.Precision.HIGH)
     return (
         product(table_real, data_real) - product(table_imag, data_imag),
         product(table_real, data_imag) + product(table_imag, data_real),
@@ -89,7 +89,7 @@
     period = freqs * tokens
     rank = lax.axis_index("seq")
     gathered = regroup_tokens(signal.reshape(count, blocks, width))
-    product = partial(jnp.einsum, "kp,cpq->ckq", precision=lax.Precision.HIGHEST)
+    product = partial(jnp.einsum, "kp,cpq->ckq", precision=lax.Precision.HIGH)
     anchor = rank * width
     first_real, first_imag = phase_table(blocks, blocks, 0, freqs, -1.0)
     top_row = lax.broadcasted_iota(jnp.int32, (blocks, blocks), 0) == 0
@@ -122,7 +122,7 @@
     first_column = lax.broadcasted_iota(jnp.int32, (blocks, blocks), 1) == 0
     real_weight = jnp.where(first_column, 1.0, 2.0 * cos_table)
     imag_weight = jnp.where(first_column, alternating(blocks, 0), -2.0 * sin_table)
-    product = partial(jnp.einsum, "pk,ckq->cpq", precision=lax.Precision.HIGHEST)
+    product = partial(jnp.einsum, "pk,ckq->cpq", precision=lax.Precision.HIGH)
     rebuilt = (product(real_weight, moved_real) + product(imag_weight, moved_imag)) * (1.0 / period)
     return regroup_tokens(rebuilt).reshape(count, tokens)
 

time: 212 us -> 206 us (0.972)
  blocking collectives: 72.8 us -> 69.3 us
  matrix products: 12.7 us -> 9.78 us
    all_to_all x1, blocking collectives: 43.5 us -> 40.7 us  [regroup_spectrum(): lax.all_to_all(jnp.concatenate([part_real, part_imag], axis=0), 'seq', sp...]
where the time goes in v7:
time: 206 us; the launch traced here: 205 us
  waiting for transfers between devices  79.2 us (38%)
  blocking collectives  69.3 us (34%)
  starting transfers between devices  38.5 us (19%)
  matrix products  9.78 us (5%)
  other arithmetic  3.53 us (2%)
  local copies, waits for them, and re-layouts  3.47 us (2%)
    all_to_all x1, waiting for transfers between devices, regroup_spectrum(): lax.all_to_all(jnp.concatenate([part_real, part_imag], axis=0), 'seq', sp...  42.1 us
    all_to_all x1, blocking collectives, regroup_spectrum(): lax.all_to_all(jnp.concatenate([part_real, part_imag], axis=0), 'seq', sp...  40.7 us
    all_to_all x1, waiting for transfers between devices, regroup_tokens(): lax.all_to_all(signal, 'seq', split_axis=1, concat_axis=1, tiled=True)  31.5 us
    all_to_all x1, blocking collectives, regroup_tokens(): lax.all_to_all(signal, 'seq', split_axis=1, concat_axis=1, tiled=True)  28.6 us
    all_to_all x1, starting transfers between devices, regroup_tokens(): lax.all_to_all(signal, 'seq', split_axis=1, concat_axis=1, tiled=True)  24 us
    all_to_all x1, starting transfers between devices, regroup_spectrum(): lax.all_to_all(jnp.concatenate([part_real, part_imag], axis=0), 'seq', sp...  8.89 us
    all_to_all x1, waiting for transfers between devices, on_device(): lax.all_to_all(copies, 'chan', split_axis=0, concat_axis=0, tiled=True)  5.69 us
    all_to_all x1, starting transfers between devices, on_device(): lax.all_to_all(copies, 'chan', split_axis=0, concat_axis=0, tiled=True)  5.55 us
  transfers between devices with their start and end apart: 3, of which 3 were waited for; matrix products, arithmetic and copies ran while one was open for 1% of the time, Pallas kernels for 0%

profile of v7, /device:TPU:16, one launch (start us, length us, event | category | flops | bytes accessed | tf_op | source)
XLA Modules:
  0.0 205.0 jit_solution(12065234896469039307)
XLA Ops:
  0.6 1.4 broadcast_in_dim.10
  2.0 5.5 %all-to-all-start = ((f32[16,4,512]{2,1,0:T(4,128)}), f32[16,4,512]{2,1,0:T(4,128)S(1)}, u32[]{:S(2)}, u32[]{:S(2)}) async-start(f32[16,4,512]{2,1,0:T(4,128)} %broadcast_in_dim.10), calls=%async_computation | async-start | bytes 262144 | tf_op jit(solution)/shard_map/all_to_all | solution.py:160
  7.6 1.0 multiply_bitcast_fusion
  8.6 5.7 %all-to-all-done = f32[16,4,512]{2,1,0:T(4,128)S(1)} async-done(((f32[16,4,512]{2,1,0:T(4,128)}), f32[16,4,512]{2,1,0:T(4,128)S(1)}, u32[]{:S(2)}, u32[]{:S(2)}) %all-to-all-start) | async-done | bytes 131104 | tf_op jit(solution)/shard_map/all_to_all | solution.py:160
  14.3 0.9 pad_maximum_fusion.1
  15.2 24.0 %all-to-all-start.1 = ((f32[12,64,128]{2,0,1:T(8,128)}), f32[12,64,128]{2,0,1:T(8,128)S(1)}, u32[]{:S(2)}, u32[]{:S(2)}) async-start(f32[12,64,128]{2,0,1:T(8,128)} %pad_maximum_fusion.1), calls=%async_computation.1 | async-start | bytes 1048576 | tf_op jit(solution)/shard_map/all_to_all | solution.py:27
  39.4 31.5 %all-to-all-done.1 = f32[12,64,128]{2,0,1:T(8,128)S(1)} async-done(((f32[12,64,128]{2,0,1:T(8,128)}), f32[12,64,128]{2,0,1:T(8,128)S(1)}, u32[]{:S(2)}, u32[]{:S(2)}) %all-to-all-start.1) | async-done | bytes 393248 | tf_op jit(solution)/shard_map/all_to_all | solution.py:27
  71.4 0.6 multiply_subtract_fusion.7
  72.1 1.3 copy.10
  73.4 8.9 %all-to-all-start.2 = ((f32[24,64,128]{2,0,1:T(8,128)}), f32[24,64,128]{2,0,1:T(8,128)S(1)}, u32[]{:S(2)}, u32[]{:S(2)}) async-start(f32[24,64,128]{2,0,1:T(8,128)} %copy.10), calls=%async_computation.2 | async-start | bytes 1572864 | tf_op jit(solution)/shard_map/all_to_all | solution.py:32
  82.8 42.1 %all-to-all-done.2 = f32[24,64,128]{2,0,1:T(8,128)S(1)} async-done(((f32[24,64,128]{2,0,1:T(8,128)}), f32[24,64,128]{2,0,1:T(8,128)S(1)}, u32[]{:S(2)}, u32[]{:S(2)}) %all-to-all-start.2) | async-done | bytes 786464 | tf_op jit(solution)/shard_map/all_to_all | solution.py:32
  125.6 0.5 fusion.176
  126.1 0.5 fusion.160
  127.0 0.6 fusion.166
  127.6 0.6 fusion.170
  128.2 0.6 convolution_add_fusion.4
  128.8 0.6 convolution_subtract_fusion.4
  129.4 0.5 fusion.184
  129.9 0.5 fusion.183
  130.4 0.5 convolution_subtract_fusion.7
  130.9 0.5 convolution_add_fusion.8
  133.8 40.7 %all_to_all.25 = f32[16,64,128]{2,0,1:T(8,128)S(1)} all-to-all(f32[16,64,128]{2,0,1:T(8,128)S(1)} %copy.13), channel_id=1, replica_groups=mesh['seq'=64,'chan'=16] {'seq'}, dimensions={1} | all-to-all | bytes 1048576 | tf_op jit(solution)/shard_map/all_to_all | solution.py:32
  175.6 28.6 %all_to_all.26 = f32[8,64,128]{2,0,1:T(8,128)S(1)} all-to-all(f32[8,64,128]{2,0,1:T(8,128)S(1)} %copy.16), channel_id=1, replica_groups=mesh['seq'=64,'chan'=16] {'seq'}, dimensions={1} | all-to-all | bytes 524288 | tf_op jit(solution)/shard_map/all_to_all | solution.py:27
  204.2 0.8 fusion.190
  (34 shorter events, 5.8 us)
Async XLA Ops:
  0.6 7.0 %copy-start.2 = (f32[4,8192]{1,0:T(4,128)S(1)}, f32[4,8192]{1,0:T(4,128)}, u32[]{:S(2)}) copy-start(f32[4,8192]{1,0:T(4,128)} %param.9) | copy-start | bytes 393220
  2.0 5.6 %copy-start = (f32[4,8192]{1,0:T(4,128)S(1)}, f32[4,8192]{1,0:T(4,128)}, u32[]{:S(2)}) copy-start(f32[4,8192]{1,0:T(4,128)} %param.8) | copy-start | bytes 393220
  2.0 5.6 %copy-start.1 = (f32[4,8192]{1,0:T(4,128)S(1)}, f32[4,8192]{1,0:T(4,128)}, u32[]{:S(2)}) copy-start(f32[4,8192]{1,0:T(4,128)} %param.11) | copy-start | bytes 393220
  2.0 12.3 %all-to-all-start = ((f32[16,4,512]{2,1,0:T(4,128)}), f32[16,4,512]{2,1,0:T(4,128)S(1)}, u32[]{:S(2)}, u32[]{:S(2)}) async-start(f32[16,4,512]{2,1,0:T(4,128)} %broadcast_in_dim.10), calls=%async_computation | async-start | bytes 262144 | tf_op jit(solution)/shard_map/all_to_all | solution.py:160
  15.2 55.7 %all-to-all-start.1 = ((f32[12,64,128]{2,0,1:T(8,128)}), f32[12,64,128]{2,0,1:T(8,128)S(1)}, u32[]{:S(2)}, u32[]{:S(2)}) async-start(f32[12,64,128]{2,0,1:T(8,128)} %pad_maximum_fusion.1), calls=%async_computation.1 | async-start | bytes 1048576 | tf_op jit(solution)/shard_map/all_to_all | solution.py:27
  73.4 51.5 %all-to-all-start.2 = ((f32[24,64,128]{2,0,1:T(8,128)}), f32[24,64,128]{2,0,1:T(8,128)S(1)}, u32[]{:S(2)}, u32[]{:S(2)}) async-start(f32[24,64,128]{2,0,1:T(8,128)} %copy.10), calls=%async_computation.2 | async-start | bytes 1572864 | tf_op jit(solution)/shard_map/all_to_all | solution.py:32

commit v8 on v7

--- a/solution.py
+++ b/solution.py
@@ -16,7 +16,7 @@
 
 
 def complex_mix(formula, table_real, table_imag, data_real, data_imag):
-    product = partial(jnp.einsum, formula, precision=lax.Precision.HIGH)
+    product = partial(jnp.einsum, formula, precision=lax.Precision.HIGHEST)
     return (
         product(table_real, data_real) - product(table_imag, data_imag),
         product(table_real, data_imag) + product(table_imag, data_real),

time: 206 us -> 211 us (1.024)
  blocking collectives: 69.3 us -> 72.6 us
  matrix products: 9.78 us -> 12.1 us
    all_to_all x1, blocking collectives: 40.7 us -> 43.3 us  [regroup_spectrum(): lax.all_to_all(jnp.concatenate([part_real, part_imag], axis=0), 'seq', sp...]
where the time goes in v8:
time: 211 us
  waiting for transfers between devices  79.2 us (38%)
  blocking collectives  72.6 us (34%)
  starting transfers between devices  38.5 us (18%)
  matrix products  12.1 us (6%)
  other arithmetic  3.53 us (2%)
  local copies, waits for them, and re-layouts  3.47 us (2%)
    all_to_all x1, blocking collectives, regroup_spectrum(): lax.all_to_all(jnp.concatenate([part_real, part_imag], axis=0), 'seq', sp...  43.3 us
    all_to_all x1, waiting for transfers between devices, regroup_spectrum(): lax.all_to_all(jnp.concatenate([part_real, part_imag], axis=0), 'seq', sp...  42.1 us
    all_to_all x1, waiting for transfers between devices, regroup_tokens(): lax.all_to_all(signal, 'seq', split_axis=1, concat_axis=1, tiled=True)  31.5 us
    all_to_all x1, blocking collectives, regroup_tokens(): lax.all_to_all(signal, 'seq', split_axis=1, concat_axis=1, tiled=True)  29.3 us
    all_to_all x1, starting transfers between devices, regroup_tokens(): lax.all_to_all(signal, 'seq', split_axis=1, concat_axis=1, tiled=True)  24 us
    all_to_all x1, starting transfers between devices, regroup_spectrum(): lax.all_to_all(jnp.concatenate([part_real, part_imag], axis=0), 'seq', sp...  8.9 us
    all_to_all x1, waiting for transfers between devices, on_device(): lax.all_to_all(copies, 'chan', split_axis=0, concat_axis=0, tiled=True)  5.69 us
    all_to_all x1, starting transfers between devices, on_device(): lax.all_to_all(copies, 'chan', split_axis=0, concat_axis=0, tiled=True)  5.55 us
  transfers between devices with their start and end apart: 3, of which 3 were waited for; matrix products, arithmetic and copies ran while one was open for 1% of the time, Pallas kernels for 0%

profile of v8, /device:TPU:16, one launch (start us, length us, event | category | flops | bytes accessed | tf_op | source)
XLA Modules:
  0.0 210.6 jit_solution(14883475531480519121)
XLA Ops:
  0.6 1.4 broadcast_in_dim.10
  2.0 5.5 %all-to-all-start = ((f32[16,4,512]{2,1,0:T(4,128)}), f32[16,4,512]{2,1,0:T(4,128)S(1)}, u32[]{:S(2)}, u32[]{:S(2)}) async-start(f32[16,4,512]{2,1,0:T(4,128)} %broadcast_in_dim.10), calls=%async_computation | async-start | bytes 262144 | tf_op jit(solution)/shard_map/all_to_all | solution.py:160
  7.6 1.0 multiply_bitcast_fusion
  8.6 5.7 %all-to-all-done = f32[16,4,512]{2,1,0:T(4,128)S(1)} async-done(((f32[16,4,512]{2,1,0:T(4,128)}), f32[16,4,512]{2,1,0:T(4,128)S(1)}, u32[]{:S(2)}, u32[]{:S(2)}) %all-to-all-start) | async-done | bytes 131104 | tf_op jit(solution)/shard_map/all_to_all | solution.py:160
  14.3 0.9 pad_maximum_fusion.1
  15.2 24.0 %all-to-all-start.1 = ((f32[12,64,128]{2,0,1:T(8,128)}), f32[12,64,128]{2,0,1:T(8,128)S(1)}, u32[]{:S(2)}, u32[]{:S(2)}) async-start(f32[12,64,128]{2,0,1:T(8,128)} %pad_maximum_fusion.1), calls=%async_computation.1 | async-start | bytes 1048576 | tf_op jit(solution)/shard_map/all_to_all | solution.py:27
  39.4 31.5 %all-to-all-done.1 = f32[12,64,128]{2,0,1:T(8,128)S(1)} async-done(((f32[12,64,128]{2,0,1:T(8,128)}), f32[12,64,128]{2,0,1:T(8,128)S(1)}, u32[]{:S(2)}, u32[]{:S(2)}) %all-to-all-start.1) | async-done | bytes 393248 | tf_op jit(solution)/shard_map/all_to_all | solution.py:27
  72.1 1.3 copy.10
  73.4 8.9 %all-to-all-start.2 = ((f32[24,64,128]{2,0,1:T(8,128)}), f32[24,64,128]{2,0,1:T(8,128)S(1)}, u32[]{:S(2)}, u32[]{:S(2)}) async-start(f32[24,64,128]{2,0,1:T(8,128)} %copy.10), calls=%async_computation.2 | async-start | bytes 1572864 | tf_op jit(solution)/shard_map/all_to_all | solution.py:32
  82.8 42.1 %all-to-all-done.2 = f32[24,64,128]{2,0,1:T(8,128)S(1)} async-done(((f32[24,64,128]{2,0,1:T(8,128)}), f32[24,64,128]{2,0,1:T(8,128)S(1)}, u32[]{:S(2)}, u32[]{:S(2)}) %all-to-all-start.2) | async-done | bytes 786464 | tf_op jit(solution)/shard_map/all_to_all | solution.py:32
  125.1 0.6 fusion.172
  125.7 0.7 fusion.176
  126.4 0.7 fusion.160
  127.1 0.6 fusion.161
  127.7 0.7 fusion.166
  128.5 0.7 fusion.170
  129.2 0.7 convolution_add_fusion.4
  129.9 0.7 convolution_subtract_fusion.4
  130.7 0.6 fusion.184
  131.9 0.6 convolution_subtract_fusion.7
  135.1 0.6 multiply_subtract_fusion.8
  136.1 43.3 %all_to_all.25 = f32[16,64,128]{2,0,1:T(8,128)S(1)} all-to-all(f32[16,64,128]{2,0,1:T(8,128)S(1)} %copy.13), channel_id=1, replica_groups=mesh['seq'=64,'chan'=16] {'seq'}, dimensions={1} | all-to-all | bytes 1048576 | tf_op jit(solution)/shard_map/all_to_all | solution.py:32
  180.4 29.3 %all_to_all.26 = f32[8,64,128]{2,0,1:T(8,128)S(1)} all-to-all(f32[8,64,128]{2,0,1:T(8,128)S(1)} %copy.16), channel_id=1, replica_groups=mesh['seq'=64,'chan'=16] {'seq'}, dimensions={1} | all-to-all | bytes 524288 | tf_op jit(solution)/shard_map/all_to_all | solution.py:27
  209.7 0.8 fusion.190
  (34 shorter events, 6.6 us)
Async XLA Ops:
  0.6 7.0 %copy-start.2 = (f32[4,8192]{1,0:T(4,128)S(1)}, f32[4,8192]{1,0:T(4,128)}, u32[]{:S(2)}) copy-start(f32[4,8192]{1,0:T(4,128)} %param.9) | copy-start | bytes 393220
  2.0 5.6 %copy-start = (f32[4,8192]{1,0:T(4,128)S(1)}, f32[4,8192]{1,0:T(4,128)}, u32[]{:S(2)}) copy-start(f32[4,8192]{1,0:T(4,128)} %param.8) | copy-start | bytes 393220
  2.0 5.6 %copy-start.1 = (f32[4,8192]{1,0:T(4,128)S(1)}, f32[4,8192]{1,0:T(4,128)}, u32[]{:S(2)}) copy-start(f32[4,8192]{1,0:T(4,128)} %param.11) | copy-start | bytes 393220
  2.0 12.3 %all-to-all-start = ((f32[16,4,512]{2,1,0:T(4,128)}), f32[16,4,512]{2,1,0:T(4,128)S(1)}, u32[]{:S(2)}, u32[]{:S(2)}) async-start(f32[16,4,512]{2,1,0:T(4,128)} %broadcast_in_dim.10), calls=%async_computation | async-start | bytes 262144 | tf_op jit(solution)/shard_map/all_to_all | solution.py:160
  15.2 55.7 %all-to-all-start.1 = ((f32[12,64,128]{2,0,1:T(8,128)}), f32[12,64,128]{2,0,1:T(8,128)S(1)}, u32[]{:S(2)}, u32[]{:S(2)}) async-start(f32[12,64,128]{2,0,1:T(8,128)} %pad_maximum_fusion.1), calls=%async_computation.1 | async-start | bytes 1048576 | tf_op jit(solution)/shard_map/all_to_all | solution.py:27
  73.4 51.5 %all-to-all-start.2 = ((f32[24,64,128]{2,0,1:T(8,128)}), f32[24,64,128]{2,0,1:T(8,128)S(1)}, u32[]{:S(2)}, u32[]{:S(2)}) async-start(f32[24,64,128]{2,0,1:T(8,128)} %copy.10), calls=%async_computation.2 | async-start | bytes 1572864 | tf_op jit(solution)/shard_map/all_to_all | solution.py:32
